TPU v7x, 32 devices: a whole 2x2x4 slice. The times are simulated.
32 devices in a mesh: tm: 8 (over z, x), space: 4 (over y, core).
Axes of the slice: x: 2, y: 2, z: 4, core: 2. Of those that a mesh axis runs over, the one named last changes fastest.
Arguments:
- video: bfloat16 [128, 4, 32, 128], P('tm', 'space'), may hold values from -6 to 6
- stem_weight: float32 [9, 16], replicated, may hold values from -2 to 2
- stem_bias: float32 [16], replicated, may hold values from -3 to 3
- spatial_weight: bfloat16 [2, 9, 16, 16], replicated, may hold values from -0.5 to 0.5
- temporal_weight: bfloat16 [2, 3, 16, 16], replicated, may hold values from -0.875 to 0.875
- temporal_bias: float32 [2, 16], replicated, may hold values from -3 to 3
- head_weight: float32 [16], replicated, may hold values from -1.5 to 1.5
- head_bias: float32 [1], replicated, may hold values from -3 to 3
Outputs:
- response: float32 [128, 4, 32, 128], P('tm', 'space')
All inputs are finite; a program needn't handle non-finite values.
Results may differ from a plain program's by a relative error of at most 0.013.
Values may be sent and summed in bfloat16 or wider, within the bound.
No kernel may reach another device: no remote copies, remote signals or barrier semaphores. Data moves between devices by JAX's collectives and lax.ppermute only.
A program may use at most 256 MiB of HBM per device.

v0:
```python
import jax
import jax.numpy as jnp
from jax import lax
from jax.experimental import pallas as pl
from jax.experimental.pallas import tpu as pltpu
from jax.sharding import PartitionSpec as P

HALO = 3
LEAD = 4


def shifted(value, axis, steps):
    count = lax.axis_size(axis)
    leading, last = (max(0, -steps), min(count, count - steps))
    if leading >= last:
        return jnp.zeros_like(value)
    return lax.ppermute(value, axis, [(source, source + steps) for source in range(leading, last)])


def grid_shape():
    parts = lax.axis_size("space")
    grid_w = min(4, parts)
    return parts // grid_w, grid_w


def spread(field, width):
    grid_w = grid_shape()[1]
    column = lax.axis_index("space") % grid_w
    west_piece = field[..., -width:]
    east_piece = field[..., :width]
    west_piece = jnp.where(column < grid_w - 1, west_piece, jnp.zeros_like(west_piece))
    east_piece = jnp.where(column > 0, east_piece, jnp.zeros_like(east_piece))
    west = shifted(west_piece, "space", 1)
    east = shifted(east_piece, "space", -1)
    wide = jnp.concatenate([west, field, east], axis=-1)
    north = shifted(wide[..., -width:, :], "space", grid_w)
    south = shifted(wide[..., :width, :], "space", -grid_w)
    return jnp.concatenate([north, wide, south], axis=-2)


def round_up(value, step):
    return (value + step - 1) // step * step


def flat_masks(height, width, length):
    grid_h, grid_w = grid_shape()
    place = lax.axis_index("space")
    pitch = width + 2 * HALO
    q = jnp.arange(length)
    y = q // pitch - HALO
    x = q % pitch - HALO
    gy = place // grid_w * height + y
    gx = place % grid_w * width + x
    inside = (q < (height + 2 * HALO) * pitch) & (gy >= 0) & (gy < grid_h * height)
    inside = inside & (gx >= 0) & (gx < grid_w * width)
    rows = []
    for margin in (2, 1):
        keep = inside & (y >= -margin) & (y < height + margin) & (x >= -margin) & (x < width + margin)
        rows.append(keep.astype(jnp.float32))
    return jnp.stack(rows)[:, None, :]


def make_kernel(n_in, count, pitch, length, base, total):
    offs = [(dy - 1) * pitch + (dx - 1) for dy in range(3) for dx in range(3)]
    shifts = [(-(base + off)) % total for off in offs]

    def kernel(first_ref, vp_ref, mask_ref, wst_ref, bst_ref, wsp_ref, tw_ref, tb_ref, hw_ref, hb_ref,
               out_ref, ha_ref, hb2_ref, s_ref):
        first = first_ref[0]
        zeros_side = jnp.zeros((ha_ref.shape[1], base), jnp.bfloat16)

        def clear(ref, n):
            def body(f, carry):
                ref[f, :, 0:base] = zeros_side
                ref[f, :, base + length:total] = zeros_side
                return carry
            lax.fori_loop(0, n, body, 0)

        clear(ha_ref, n_in)
        clear(hb2_ref, n_in - 2)

        mask0 = mask_ref[0] > 0.5
        mask1 = mask_ref[1] > 0.5

        filler = jnp.zeros((16 - len(shifts), length), jnp.float32)

        def stem(f, carry):
            v = vp_ref[f]
            rows = [pltpu.roll(v, sh, 1)[:, :length] if sh else v[:, :length] for sh in shifts]
            patch = jnp.concatenate(rows + [filler], axis=0).astype(jnp.bfloat16)
            patch = jnp.concatenate([patch, patch], axis=0)
            acc = jnp.dot(wst_ref[...], patch, preferred_element_type=jnp.float32)
            h0 = jnp.maximum(acc + bst_ref[...], 0.0).astype(jnp.bfloat16)
            keep = mask0 & (first + f >= 0)
            ha_ref[f, :, base:base + length] = jnp.where(keep, h0, jnp.zeros_like(h0))
            return carry

        lax.fori_loop(0, n_in, stem, 0)

        def spatial(block, src_ref, n):
            def body(f, carry):
                x = src_ref[f]
                pieces = [pltpu.roll(x, sh, 1)[:, :length] if sh else x[:, :length] for sh in shifts]
                patches = jnp.concatenate(pieces, axis=0)
                acc = jnp.dot(wsp_ref[block], patches, preferred_element_type=jnp.float32)
                s_ref[f] = acc.astype(jnp.bfloat16)
                return carry
            lax.fori_loop(0, n, body, 0)

        def temporal(block, src_ref, k):
            stacked = jnp.concatenate([s_ref[k], s_ref[k + 1], s_ref[k + 2]], axis=0)
            acc = jnp.dot(tw_ref[block], stacked, preferred_element_type=jnp.float32) + tb_ref[block]
            centre = src_ref[k + 2, :, base:base + length].astype(jnp.float32)
            return (centre + jnp.maximum(acc, 0.0)).astype(jnp.bfloat16)

        spatial(0, ha_ref, n_in)

        def block0(k, carry):
            h1 = temporal(0, ha_ref, k)
            keep = mask1 & (first + 2 + k >= 0)
            hb2_ref[k, :, base:base + length] = jnp.where(keep, h1, jnp.zeros_like(h1))
            return carry

        lax.fori_loop(0, n_in - 2, block0, 0)
        spatial(1, hb2_ref, n_in - 2)

        def block1(k, carry):
            h2 = temporal(1, hb2_ref, k).astype(jnp.float32)
            head = jnp.sum(hw_ref[...] * h2, axis=0, keepdims=True) + hb_ref[...]
            out_ref[k] = head
            return carry

        lax.fori_loop(0, count, block1, 0)

    return kernel


def shards(video, stem_weight, stem_bias, spatial_weight, temporal_weight, temporal_bias, head_weight, head_bias):
    clip = video[:, 0]
    count, height, width = clip.shape
    lead = shifted(clip[-LEAD:], "tm", 1)
    extended = spread(jnp.concatenate([lead, clip], axis=0), HALO)
    n_in = count + LEAD
    pitch = width + 2 * HALO
    rows = height + 2 * HALO
    length = round_up(rows * pitch, 128)
    base = round_up(pitch + 1, 128)
    total = length + 2 * base
    flat = extended.reshape(n_in, rows * pitch)
    flat = jnp.pad(flat.astype(jnp.float32), ((0, 0), (base, total - base - rows * pitch)))
    vp = flat[:, None, :]

    channels = stem_weight.shape[1]
    w_hi = stem_weight.astype(jnp.bfloat16)
    w_lo = (stem_weight - w_hi.astype(jnp.float32)).astype(jnp.bfloat16)
    wst = jnp.zeros((channels, 32), jnp.bfloat16)
    wst = wst.at[:, 0:9].set(w_hi.T).at[:, 16:25].set(w_lo.T)
    bst = stem_bias.astype(jnp.float32)[:, None]
    wsp = spatial_weight.transpose(0, 2, 1, 3).reshape(2, channels, 9 * channels)
    tw = temporal_weight.transpose(0, 2, 1, 3).reshape(2, channels, 3 * channels)
    tb = temporal_bias.astype(jnp.float32)[:, :, None]
    hw = head_weight.astype(jnp.float32)[:, None]
    hb = head_bias.astype(jnp.float32).reshape(1, 1)
    masks = flat_masks(height, width, length)
    first = (lax.axis_index("tm") * count - LEAD).astype(jnp.int32).reshape(1)

    vmem = pltpu.MemorySpace.VMEM if hasattr(pltpu, "MemorySpace") else pltpu.TPUMemorySpace.VMEM
    smem = pltpu.MemorySpace.SMEM if hasattr(pltpu, "MemorySpace") else pltpu.TPUMemorySpace.SMEM
    spec = pl.BlockSpec(memory_space=vmem)
    out = pl.pallas_call(
        make_kernel(n_in, count, pitch, length, base, total),
        out_shape=jax.ShapeDtypeStruct((count, 1, length), jnp.float32),
        in_specs=[pl.BlockSpec(memory_space=smem)] + [spec] * 9,
        out_specs=spec,
        scratch_shapes=[
            pltpu.VMEM((n_in, channels, total), jnp.bfloat16),
            pltpu.VMEM((n_in - 2, channels, total), jnp.bfloat16),
            pltpu.VMEM((n_in, channels, length), jnp.bfloat16),
        ],
        compiler_params=pltpu.CompilerParams(vmem_limit_bytes=48 * 1024 * 1024),
    )(first, vp, masks, wst, bst, wsp, tw, tb, hw, hb)
    result = out[:, 0, : rows * pitch].reshape(count, rows, pitch)
    result = result[:, HALO:HALO + height, HALO:HALO + width]
    return result[:, None]


def solution(mesh):
    placed = (P("tm", "space", None, None), P(), P(), P(), P(), P(), P(), P())
    return jax.shard_map(
        shards, mesh=mesh, in_specs=placed, out_specs=P("tm", "space", None, None), check_vma=False
    )
```

profile of v0, /device:TPU:1, one launch (start us, length us, event | category | flops | bytes accessed | tf_op | source)
XLA Modules:
  0.0 58.4 jit_solution(11250442762458403475)
XLA Ops:
  0.0 0.0 copy-start
  0.0 0.8 %slice_bitcast_fusion.1 = bf16[4,32,128]{2,1,0:T(8,128)(2,1)S(1)} fusion(bf16[16,1,32,128]{3,2,0,1:T(8,128)(2,1)} %bitcast.21), kind=kLoop, calls=%fused_computation.16 | loop fusion | bytes 65536 | tf_op jit(solution)/shard_map/slice | solution.py:141
  0.8 3.9 %collective-permute-start = (bf16[4,32,128]{2,1,0:T(8,128)(2,1)S(1)}, bf16[4,32,128]{2,1,0:T(8,128)(2,1)S(1)}, u32[]{:S(2)}, u32[]{:S(2)}) collective-permute-start(bf16[4,32,128]{2,1,0:T(8,128)(2,1)S(1)} %slice_bitcast_fusion.1), channel_id=1, source_target_pairs={{0,4},{4,8},{8,12},{12,16},{16,20},{20,24},{24,28},{1,5},{5,9},{9,... | collective-permute-start | bytes 98312 | tf_op jit(solution)/shard_map/ppermute | solution.py:17
  4.8 0.3 compare_and_fusion
  5.1 0.0 copy-start.3
  5.1 0.1 add_convert_fusion
  5.2 0.6 %copy-done.3 = f32[9,16]{1,0:T(8,128)S(1)} copy-done((f32[9,16]{1,0:T(8,128)S(1)}, f32[9,16]{1,0:T(8,128)}, u32[]{:S(2)}) %copy-start.3) | copy-done | bytes 600
  5.8 0.1 copy.18
  5.9 0.6 %compare_reduce_fusion.1 = pred[]{:T(512)} fusion(), kind=kLoop, calls=%fused_computation.24 | loop fusion | flops 5 | bytes 1 | tf_op jit(solution)/shard_map/reduce.2
  6.5 0.6 %compare_reduce_fusion = pred[]{:T(512)} fusion(), kind=kLoop, calls=%fused_computation.23 | loop fusion | flops 7 | bytes 1 | tf_op jit(solution)/shard_map/reduce.3
  7.2 0.0 collective-permute-done
  7.2 0.0 copy-done
  7.2 0.1 maximum_select_fusion
  7.3 0.0 copy-start.1
  7.3 4.1 %collective-permute-start.1 = (bf16[20,32,3]{2,1,0:T(8,128)(2,1)S(1)}, bf16[20,32,3]{2,1,0:T(8,128)(2,1)S(1)}, u32[]{:S(2)}, u32[]{:S(2)}) collective-permute-start(bf16[20,32,3]{2,1,0:T(8,128)(2,1)S(1)} %get-tuple-element.29), channel_id=1, source_target_pairs={{0,1},{1,2},{2,3},{4,5},{5,6},{6,7},{8,9},{9,10},{10,11},{12,13},{... | collective-permute-start | bytes 11528 | tf_op jit(solution)/shard_map/ppermute | solution.py:17
  11.4 1.9 %collective-permute-start.2 = (bf16[20,32,3]{2,1,0:T(8,128)(2,1)S(1)}, bf16[20,32,3]{2,1,0:T(8,128)(2,1)S(1)}, u32[]{:S(2)}, u32[]{:S(2)}) collective-permute-start(bf16[20,32,3]{2,1,0:T(8,128)(2,1)S(1)} %get-tuple-element.30), channel_id=1, source_target_pairs={{1,0},{2,1},{3,2},{5,4},{6,5},{7,6},{9,8},{10,9},{11,10},{13,12},{... | collective-permute-start | bytes 11528 | tf_op jit(solution)/shard_map/ppermute | solution.py:17
  13.4 1.3 %fusion.4 = (bf16[16,9]{1,0:T(8,128)(2,1)S(1)}, bf16[16,9]{1,0:T(8,128)(2,1)S(1)}) fusion(f32[9,16]{0,1:T(8,128)S(1)} %copy.18, pred[]{:T(512)} %compare_reduce_fusion, pred[]{:T(512)} %compare_reduce_fusion.1), kind=kLoop, calls=%fused_computation.21 | loop fusion | flops 864 | bytes 1154 | tf_op jit(solution)/shard_map/transpose.19
  14.7 0.0 copy-done.1
  14.7 0.1 copy.20
  14.8 0.0 copy-start.2
  14.8 0.1 copy.23.wsp_ref
  14.9 0.7 %copy-done.2 = bf16[2,3,16,16]{3,2,1,0:T(8,128)(2,1)S(1)} copy-done((bf16[2,3,16,16]{3,2,1,0:T(8,128)(2,1)S(1)}, bf16[2,3,16,16]{3,2,1,0:T(8,128)(2,1)}, u32[]{:S(2)}) %copy-start.2) | copy-done | bytes 3096
  15.6 0.1 reshape.210.tw_ref
  15.7 0.0 copy-start.4
  15.7 0.7 %copy-done.4 = f32[2,16]{1,0:T(2,128)S(1)} copy-done((f32[2,16]{1,0:T(2,128)S(1)}, f32[2,16]{1,0:T(2,128)}, u32[]{:S(2)}) %copy-start.4) | copy-done | bytes 152
  16.3 0.1 copy.24.tb_ref
  16.4 0.0 copy-start.5
  16.4 0.7 %copy-done.5 = f32[16]{0:T(128)S(1)} copy-done((f32[16]{0:T(128)S(1)}, f32[16]{0:T(128)}, u32[]{:S(2)}) %copy-start.5) | copy-done | bytes 88
  17.1 0.1 copy.22.bst_ref
  17.2 0.0 copy-start.6
  17.2 0.7 %copy-done.6 = f32[16]{0:T(128)S(1)} copy-done((f32[16]{0:T(128)S(1)}, f32[16]{0:T(128)}, u32[]{:S(2)}) %copy-start.6) | copy-done | bytes 88
  17.8 0.1 copy.25.hw_ref
  18.6 0.2 scatter.9.wst_ref
  18.8 0.0 collective-permute-done.1
  18.8 0.0 collective-permute-done.2
  18.9 0.4 pad_maximum_fusion
  19.3 0.4 convert_element_type.31
  19.7 0.3 reshape.212.vp_ref
  20.0 36.3 %shard_map.82 = f32[16,1,5120]{2,1,0:T(1,128)S(1)} custom-call(s32[1]{0:T(128)} %bitcast.first_ref, f32[20,1,5632]{2,1,0:T(1,128)S(1)} %reshape.212.vp_ref, f32[2,1,5120]{2,1,0:T(1,128)S(1)} %reshape.213.mask_ref, bf16[16,32]{1,0:T(8,128)(2,1)S(1)} %scatter.9.wst_ref, f32[16,1]{1,0:T(8,128)S(1)} %copy.22.bst_ref, bf16[2,16,144]{2,1,0:T(8,128)(2,1)S(1)} %copy.23.wsp_ref, ...), custom_call_target="tpu_custom_call" | custom-call | tf_op jit(solution)/shard_map/pallas_call | solution.py:170
  56.4 0.8 %slice_reduce_fusion = f32[16,5092]{1,0:T(8,128)S(1)} fusion(f32[16,1,5120]{2,1,0:T(1,128)S(1)} %shard_map.82), kind=kLoop, calls=%fused_computation.1 | loop fusion | bytes 651776 | tf_op jit(solution)/shard_map/slice | solution.py:182
  57.2 0.4 reshape_squeeze.3
  57.6 0.8 %slice_bitcast_fusion = f32[16,1,32,128]{3,2,1,0:T(8,128)} fusion(f32[16,38,134]{2,1,0:T(8,128)S(1)} %reshape_squeeze.3), kind=kLoop, calls=%fused_computation.3 | loop fusion | bytes 524288 | tf_op jit(solution)/shard_map/broadcast_in_dim | solution.py:184
  (5 shorter events, 0.1 us)
Async XLA Ops:
  0.0 7.2 %copy-start = (bf16[16,1,32,128]{3,2,1,0:T(8,128)(2,1)S(1)}, bf16[16,1,32,128]{3,2,1,0:T(8,128)(2,1)}, u32[]{:S(2)}) copy-start(bf16[16,1,32,128]{3,2,1,0:T(8,128)(2,1)} %param.12) | copy-start | bytes 393220
  0.8 6.3 %collective-permute-start = (bf16[4,32,128]{2,1,0:T(8,128)(2,1)S(1)}, bf16[4,32,128]{2,1,0:T(8,128)(2,1)S(1)}, u32[]{:S(2)}, u32[]{:S(2)}) collective-permute-start(bf16[4,32,128]{2,1,0:T(8,128)(2,1)S(1)} %slice_bitcast_fusion.1), channel_id=1, source_target_pairs={{0,4},{4,8},{8,12},{12,16},{16,20},{20,24},{24,28},{1,5},{5,9},{9,... | collective-permute-start | bytes 98312 | tf_op jit(solution)/shard_map/ppermute | solution.py:17
  5.1 0.7 %copy-start.3 = (f32[9,16]{1,0:T(8,128)S(1)}, f32[9,16]{1,0:T(8,128)}, u32[]{:S(2)}) copy-start(f32[9,16]{1,0:T(8,128)} %param.13) | copy-start | bytes 1732
  7.3 7.4 %copy-start.1 = (bf16[2,9,16,16]{3,2,1,0:T(8,128)(2,1)S(1)}, bf16[2,9,16,16]{3,2,1,0:T(8,128)(2,1)}, u32[]{:S(2)}) copy-start(bf16[2,9,16,16]{3,2,1,0:T(8,128)(2,1)} %param.15) | copy-start | bytes 27652
  7.3 11.5 %collective-permute-start.1 = (bf16[20,32,3]{2,1,0:T(8,128)(2,1)S(1)}, bf16[20,32,3]{2,1,0:T(8,128)(2,1)S(1)}, u32[]{:S(2)}, u32[]{:S(2)}) collective-permute-start(bf16[20,32,3]{2,1,0:T(8,128)(2,1)S(1)} %get-tuple-element.29), channel_id=1, source_target_pairs={{0,1},{1,2},{2,3},{4,5},{5,6},{6,7},{8,9},{9,10},{10,11},{12,13},{... | collective-permute-start | bytes 11528 | tf_op jit(solution)/shard_map/ppermute | solution.py:17
  11.4 7.4 %collective-permute-start.2 = (bf16[20,32,3]{2,1,0:T(8,128)(2,1)S(1)}, bf16[20,32,3]{2,1,0:T(8,128)(2,1)S(1)}, u32[]{:S(2)}, u32[]{:S(2)}) collective-permute-start(bf16[20,32,3]{2,1,0:T(8,128)(2,1)S(1)} %get-tuple-element.30), channel_id=1, source_target_pairs={{1,0},{2,1},{3,2},{5,4},{6,5},{7,6},{9,8},{10,9},{11,10},{13,12},{... | collective-permute-start | bytes 11528 | tf_op jit(solution)/shard_map/ppermute | solution.py:17
  14.8 0.7 %copy-start.2 = (bf16[2,3,16,16]{3,2,1,0:T(8,128)(2,1)S(1)}, bf16[2,3,16,16]{3,2,1,0:T(8,128)(2,1)}, u32[]{:S(2)}) copy-start(bf16[2,3,16,16]{3,2,1,0:T(8,128)(2,1)} %param.16) | copy-start | bytes 9220
  15.7 0.7 %copy-start.4 = (f32[2,16]{1,0:T(2,128)S(1)}, f32[2,16]{1,0:T(2,128)}, u32[]{:S(2)}) copy-start(f32[2,16]{1,0:T(2,128)} %param.17) | copy-start | bytes 388
  16.4 0.7 %copy-start.5 = (f32[16]{0:T(128)S(1)}, f32[16]{0:T(128)}, u32[]{:S(2)}) copy-start(f32[16]{0:T(128)} %param.14) | copy-start | bytes 196
  17.2 0.7 %copy-start.6 = (f32[16]{0:T(128)S(1)}, f32[16]{0:T(128)}, u32[]{:S(2)}) copy-start(f32[16]{0:T(128)} %param.18) | copy-start | bytes 196
where the time goes:
time: 58.9 us; the launch traced here: 58.4 us
  Pallas kernels  36.3 us (62%)
  starting transfers between devices  9.97 us (17%)
  local copies, waits for them, and re-layouts  7.78 us (13%)
  other arithmetic  3.48 us (6%)
  between operations  0.87 us (1%)
    pallas_call x1, Pallas kernels, shards(): pl.pallas_call(make_kernel(n_in, count, pitch, length, base, total), out_...  36.3 us
    ppermute x3, starting transfers between devices, shifted(): lax.ppermute(value, axis, [(source, source + steps) for source in range(l...  9.97 us
    unnamed x15, local copies, waits for them, and re-layouts  3.36 us
    another operation x3, other arithmetic  2.56 us
  transfers between devices with their start and end apart: 3, of which 0 were waited for; matrix products, arithmetic and copies ran while one was open for 7% of the time, Pallas kernels for 0%

commit v1 on v0

--- a/solution.py
+++ b/solution.py
@@ -60,74 +60,86 @@
     return jnp.stack(rows)[:, None, :]
 
 
-def make_kernel(n_in, count, pitch, length, base, total):
+def make_kernel(n_in, count, pitch, length, base, total, height):
     offs = [(dy - 1) * pitch + (dx - 1) for dy in range(3) for dx in range(3)]
     shifts = [(-(base + off)) % total for off in offs]
+
+    def span(margin):
+        lo = (HALO - margin) * pitch // 128 * 128
+        hi = min(length, round_up((HALO + height + margin) * pitch, 128))
+        return lo, hi
+
+    spans = [span(2), span(1), span(0)]
 
     def kernel(first_ref, vp_ref, mask_ref, wst_ref, bst_ref, wsp_ref, tw_ref, tb_ref, hw_ref, hb_ref,
                out_ref, ha_ref, hb2_ref, s_ref):
         first = first_ref[0]
-        zeros_side = jnp.zeros((ha_ref.shape[1], base), jnp.bfloat16)
-
-        def clear(ref, n):
+        channels = ha_ref.shape[1]
+
+        def clear(ref, n, lo, hi):
+            front = jnp.zeros((channels, base + lo), jnp.bfloat16)
+            back = jnp.zeros((channels, total - base - hi), jnp.bfloat16)
+
             def body(f, carry):
-                ref[f, :, 0:base] = zeros_side
-                ref[f, :, base + length:total] = zeros_side
+                ref[f, :, 0:base + lo] = front
+                ref[f, :, base + hi:total] = back
                 return carry
             lax.fori_loop(0, n, body, 0)
 
-        clear(ha_ref, n_in)
-        clear(hb2_ref, n_in - 2)
-
-        mask0 = mask_ref[0] > 0.5
-        mask1 = mask_ref[1] > 0.5
-
-        filler = jnp.zeros((16 - len(shifts), length), jnp.float32)
+        clear(ha_ref, n_in, *spans[0])
+        clear(hb2_ref, n_in - 2, *spans[1])
+
+        lo0, hi0 = spans[0]
+        mask0 = mask_ref[0, :, lo0:hi0] > 0.5
+        filler = jnp.zeros((16 - len(shifts), hi0 - lo0), jnp.float32)
 
         def stem(f, carry):
             v = vp_ref[f]
-            rows = [pltpu.roll(v, sh, 1)[:, :length] if sh else v[:, :length] for sh in shifts]
+            rows = [pltpu.roll(v, sh, 1)[:, lo0:hi0] if sh else v[:, lo0:hi0] for sh in shifts]
             patch = jnp.concatenate(rows + [filler], axis=0).astype(jnp.bfloat16)
             patch = jnp.concatenate([patch, patch], axis=0)
             acc = jnp.dot(wst_ref[...], patch, preferred_element_type=jnp.float32)
             h0 = jnp.maximum(acc + bst_ref[...], 0.0).astype(jnp.bfloat16)
             keep = mask0 & (first + f >= 0)
-            ha_ref[f, :, base:base + length] = jnp.where(keep, h0, jnp.zeros_like(h0))
+            ha_ref[f, :, base + lo0:base + hi0] = jnp.where(keep, h0, jnp.zeros_like(h0))
             return carry
 
         lax.fori_loop(0, n_in, stem, 0)
 
-        def spatial(block, src_ref, n):
+        def spatial(block, src_ref, n, lo, hi):
             def body(f, carry):
                 x = src_ref[f]
-                pieces = [pltpu.roll(x, sh, 1)[:, :length] if sh else x[:, :length] for sh in shifts]
+                pieces = [pltpu.roll(x, sh, 1)[:, lo:hi] if sh else x[:, lo:hi] for sh in shifts]
                 patches = jnp.concatenate(pieces, axis=0)
                 acc = jnp.dot(wsp_ref[block], patches, preferred_element_type=jnp.float32)
-                s_ref[f] = acc.astype(jnp.bfloat16)
+                s_ref[f, :, lo:hi] = acc.astype(jnp.bfloat16)
                 return carry
             lax.fori_loop(0, n, body, 0)
 
-        def temporal(block, src_ref, k):
-            stacked = jnp.concatenate([s_ref[k], s_ref[k + 1], s_ref[k + 2]], axis=0)
+        def temporal(block, src_ref, k, lo, hi):
+            stacked = jnp.concatenate([s_ref[k, :, lo:hi], s_ref[k + 1, :, lo:hi], s_ref[k + 2, :, lo:hi]], axis=0)
             acc = jnp.dot(tw_ref[block], stacked, preferred_element_type=jnp.float32) + tb_ref[block]
-            centre = src_ref[k + 2, :, base:base + length].astype(jnp.float32)
+            centre = src_ref[k + 2, :, base + lo:base + hi].astype(jnp.float32)
             return (centre + jnp.maximum(acc, 0.0)).astype(jnp.bfloat16)
 
-        spatial(0, ha_ref, n_in)
+        lo1, hi1 = spans[1]
+        spatial(0, ha_ref, n_in, lo1, hi1)
+        mask1 = mask_ref[1, :, lo1:hi1] > 0.5
 
         def block0(k, carry):
-            h1 = temporal(0, ha_ref, k)
+            h1 = temporal(0, ha_ref, k, lo1, hi1)
             keep = mask1 & (first + 2 + k >= 0)
-            hb2_ref[k, :, base:base + length] = jnp.where(keep, h1, jnp.zeros_like(h1))
+            hb2_ref[k, :, base + lo1:base + hi1] = jnp.where(keep, h1, jnp.zeros_like(h1))
             return carry
 
         lax.fori_loop(0, n_in - 2, block0, 0)
-        spatial(1, hb2_ref, n_in - 2)
+        lo2, hi2 = spans[2]
+        spatial(1, hb2_ref, n_in - 2, lo2, hi2)
 
         def block1(k, carry):
-            h2 = temporal(1, hb2_ref, k).astype(jnp.float32)
+            h2 = temporal(1, hb2_ref, k, lo2, hi2).astype(jnp.float32)
             head = jnp.sum(hw_ref[...] * h2, axis=0, keepdims=True) + hb_ref[...]
-            out_ref[k] = head
+            out_ref[k, :, lo2:hi2] = head
             return carry
 
         lax.fori_loop(0, count, block1, 0)
@@ -168,7 +180,7 @@
     smem = pltpu.MemorySpace.SMEM if hasattr(pltpu, "MemorySpace") else pltpu.TPUMemorySpace.SMEM
     spec = pl.BlockSpec(memory_space=vmem)
     out = pl.pallas_call(
-        make_kernel(n_in, count, pitch, length, base, total),
+        make_kernel(n_in, count, pitch, length, base, total, height),
         out_shape=jax.ShapeDtypeStruct((count, 1, length), jnp.float32),
         in_specs=[pl.BlockSpec(memory_space=smem)] + [spec] * 9,
         out_specs=spec,

time: 58.9 us -> 56.6 us (0.961)
  Pallas kernels: 36.3 us -> 34.1 us
    pallas_call x1, Pallas kernels: 36.3 us -> 34.1 us  [shards(): pl.pallas_call(make_kernel(n_in, count, pitch, length, base, total, heigh...]
where the time goes in v1:
time: 56.6 us; the launch traced here: 56.2 us
  Pallas kernels  34.1 us (60%)
  starting transfers between devices  9.97 us (18%)
  local copies, waits for them, and re-layouts  7.78 us (14%)
  other arithmetic  3.48 us (6%)
  between operations  0.87 us (2%)
    pallas_call x1, Pallas kernels, shards(): pl.pallas_call(make_kernel(n_in, count, pitch, length, base, total, heigh...  34.1 us
    ppermute x3, starting transfers between devices, shifted(): lax.ppermute(value, axis, [(source, source + steps) for source in range(l...  9.97 us
    unnamed x15, local copies, waits for them, and re-layouts  3.36 us
    another operation x3, other arithmetic  2.56 us
  transfers between devices with their start and end apart: 3, of which 0 were waited for; matrix products, arithmetic and copies ran while one was open for 7% of the time, Pallas kernels for 0%

profile of v1, /device:TPU:1, one launch (start us, length us, event | category | flops | bytes accessed | tf_op | source)
XLA Modules:
  0.0 56.2 jit_solution(15751758835083176080)
XLA Ops:
  0.0 0.0 copy-start
  0.0 0.8 %slice_bitcast_fusion.1 = bf16[4,32,128]{2,1,0:T(8,128)(2,1)S(1)} fusion(bf16[16,1,32,128]{3,2,0,1:T(8,128)(2,1)} %bitcast.21), kind=kLoop, calls=%fused_computation.16 | loop fusion | bytes 65536 | tf_op jit(solution)/shard_map/slice | solution.py:153
  0.8 3.9 %collective-permute-start = (bf16[4,32,128]{2,1,0:T(8,128)(2,1)S(1)}, bf16[4,32,128]{2,1,0:T(8,128)(2,1)S(1)}, u32[]{:S(2)}, u32[]{:S(2)}) collective-permute-start(bf16[4,32,128]{2,1,0:T(8,128)(2,1)S(1)} %slice_bitcast_fusion.1), channel_id=1, source_target_pairs={{0,4},{4,8},{8,12},{12,16},{16,20},{20,24},{24,28},{1,5},{5,9},{9,... | collective-permute-start | bytes 98312 | tf_op jit(solution)/shard_map/ppermute | solution.py:17
  4.8 0.3 compare_and_fusion
  5.1 0.0 copy-start.3
  5.1 0.1 add_convert_fusion
  5.2 0.6 %copy-done.3 = f32[9,16]{1,0:T(8,128)S(1)} copy-done((f32[9,16]{1,0:T(8,128)S(1)}, f32[9,16]{1,0:T(8,128)}, u32[]{:S(2)}) %copy-start.3) | copy-done | bytes 600
  5.8 0.1 copy.18
  5.9 0.6 %compare_reduce_fusion.1 = pred[]{:T(512)} fusion(), kind=kLoop, calls=%fused_computation.24 | loop fusion | flops 5 | bytes 1 | tf_op jit(solution)/shard_map/reduce.2
  6.5 0.6 %compare_reduce_fusion = pred[]{:T(512)} fusion(), kind=kLoop, calls=%fused_computation.23 | loop fusion | flops 7 | bytes 1 | tf_op jit(solution)/shard_map/reduce.3
  7.2 0.0 collective-permute-done
  7.2 0.0 copy-done
  7.2 0.1 maximum_select_fusion
  7.3 0.0 copy-start.1
  7.3 4.1 %collective-permute-start.1 = (bf16[20,32,3]{2,1,0:T(8,128)(2,1)S(1)}, bf16[20,32,3]{2,1,0:T(8,128)(2,1)S(1)}, u32[]{:S(2)}, u32[]{:S(2)}) collective-permute-start(bf16[20,32,3]{2,1,0:T(8,128)(2,1)S(1)} %get-tuple-element.29), channel_id=1, source_target_pairs={{0,1},{1,2},{2,3},{4,5},{5,6},{6,7},{8,9},{9,10},{10,11},{12,13},{... | collective-permute-start | bytes 11528 | tf_op jit(solution)/shard_map/ppermute | solution.py:17
  11.4 1.9 %collective-permute-start.2 = (bf16[20,32,3]{2,1,0:T(8,128)(2,1)S(1)}, bf16[20,32,3]{2,1,0:T(8,128)(2,1)S(1)}, u32[]{:S(2)}, u32[]{:S(2)}) collective-permute-start(bf16[20,32,3]{2,1,0:T(8,128)(2,1)S(1)} %get-tuple-element.30), channel_id=1, source_target_pairs={{1,0},{2,1},{3,2},{5,4},{6,5},{7,6},{9,8},{10,9},{11,10},{13,12},{... | collective-permute-start | bytes 11528 | tf_op jit(solution)/shard_map/ppermute | solution.py:17
  13.4 1.3 %fusion.4 = (bf16[16,9]{1,0:T(8,128)(2,1)S(1)}, bf16[16,9]{1,0:T(8,128)(2,1)S(1)}) fusion(f32[9,16]{0,1:T(8,128)S(1)} %copy.18, pred[]{:T(512)} %compare_reduce_fusion, pred[]{:T(512)} %compare_reduce_fusion.1), kind=kLoop, calls=%fused_computation.21 | loop fusion | flops 864 | bytes 1154 | tf_op jit(solution)/shard_map/transpose.19
  14.7 0.0 copy-done.1
  14.7 0.1 copy.20
  14.8 0.0 copy-start.2
  14.8 0.1 copy.23.wsp_ref
  14.9 0.7 %copy-done.2 = bf16[2,3,16,16]{3,2,1,0:T(8,128)(2,1)S(1)} copy-done((bf16[2,3,16,16]{3,2,1,0:T(8,128)(2,1)S(1)}, bf16[2,3,16,16]{3,2,1,0:T(8,128)(2,1)}, u32[]{:S(2)}) %copy-start.2) | copy-done | bytes 3096
  15.6 0.1 reshape.210.tw_ref
  15.7 0.0 copy-start.4
  15.7 0.7 %copy-done.4 = f32[2,16]{1,0:T(2,128)S(1)} copy-done((f32[2,16]{1,0:T(2,128)S(1)}, f32[2,16]{1,0:T(2,128)}, u32[]{:S(2)}) %copy-start.4) | copy-done | bytes 152
  16.3 0.1 copy.24.tb_ref
  16.4 0.0 copy-start.5
  16.4 0.7 %copy-done.5 = f32[16]{0:T(128)S(1)} copy-done((f32[16]{0:T(128)S(1)}, f32[16]{0:T(128)}, u32[]{:S(2)}) %copy-start.5) | copy-done | bytes 88
  17.1 0.1 copy.22.bst_ref
  17.2 0.0 copy-start.6
  17.2 0.7 %copy-done.6 = f32[16]{0:T(128)S(1)} copy-done((f32[16]{0:T(128)S(1)}, f32[16]{0:T(128)}, u32[]{:S(2)}) %copy-start.6) | copy-done | bytes 88
  17.8 0.1 copy.25.hw_ref
  18.6 0.2 scatter.9.wst_ref
  18.8 0.0 collective-permute-done.1
  18.8 0.0 collective-permute-done.2
  18.9 0.4 pad_maximum_fusion
  19.3 0.4 convert_element_type.31
  19.7 0.3 reshape.212.vp_ref
  20.0 34.1 %shard_map.82 = f32[16,1,5120]{2,1,0:T(1,128)S(1)} custom-call(s32[1]{0:T(128)} %bitcast.first_ref, f32[20,1,5632]{2,1,0:T(1,128)S(1)} %reshape.212.vp_ref, f32[2,1,5120]{2,1,0:T(1,128)S(1)} %reshape.213.mask_ref, bf16[16,32]{1,0:T(8,128)(2,1)S(1)} %scatter.9.wst_ref, f32[16,1]{1,0:T(8,128)S(1)} %copy.22.bst_ref, bf16[2,16,144]{2,1,0:T(8,128)(2,1)S(1)} %copy.23.wsp_ref, ...), custom_call_target="tpu_custom_call" | custom-call | tf_op jit(solution)/shard_map/pallas_call | solution.py:182
  54.1 0.8 %slice_reduce_fusion = f32[16,5092]{1,0:T(8,128)S(1)} fusion(f32[16,1,5120]{2,1,0:T(1,128)S(1)} %shard_map.82), kind=kLoop, calls=%fused_computation.1 | loop fusion | bytes 651776 | tf_op jit(solution)/shard_map/slice | solution.py:194
  55.0 0.4 reshape_squeeze.3
  55.4 0.8 %slice_bitcast_fusion = f32[16,1,32,128]{3,2,1,0:T(8,128)} fusion(f32[16,38,134]{2,1,0:T(8,128)S(1)} %reshape_squeeze.3), kind=kLoop, calls=%fused_computation.3 | loop fusion | bytes 524288 | tf_op jit(solution)/shard_map/broadcast_in_dim | solution.py:196
  (5 shorter events, 0.1 us)
Async XLA Ops:
  0.0 7.2 %copy-start = (bf16[16,1,32,128]{3,2,1,0:T(8,128)(2,1)S(1)}, bf16[16,1,32,128]{3,2,1,0:T(8,128)(2,1)}, u32[]{:S(2)}) copy-start(bf16[16,1,32,128]{3,2,1,0:T(8,128)(2,1)} %param.12) | copy-start | bytes 393220
  0.8 6.3 %collective-permute-start = (bf16[4,32,128]{2,1,0:T(8,128)(2,1)S(1)}, bf16[4,32,128]{2,1,0:T(8,128)(2,1)S(1)}, u32[]{:S(2)}, u32[]{:S(2)}) collective-permute-start(bf16[4,32,128]{2,1,0:T(8,128)(2,1)S(1)} %slice_bitcast_fusion.1), channel_id=1, source_target_pairs={{0,4},{4,8},{8,12},{12,16},{16,20},{20,24},{24,28},{1,5},{5,9},{9,... | collective-permute-start | bytes 98312 | tf_op jit(solution)/shard_map/ppermute | solution.py:17
  5.1 0.7 %copy-start.3 = (f32[9,16]{1,0:T(8,128)S(1)}, f32[9,16]{1,0:T(8,128)}, u32[]{:S(2)}) copy-start(f32[9,16]{1,0:T(8,128)} %param.13) | copy-start | bytes 1732
  7.3 7.4 %copy-start.1 = (bf16[2,9,16,16]{3,2,1,0:T(8,128)(2,1)S(1)}, bf16[2,9,16,16]{3,2,1,0:T(8,128)(2,1)}, u32[]{:S(2)}) copy-start(bf16[2,9,16,16]{3,2,1,0:T(8,128)(2,1)} %param.15) | copy-start | bytes 27652
  7.3 11.5 %collective-permute-start.1 = (bf16[20,32,3]{2,1,0:T(8,128)(2,1)S(1)}, bf16[20,32,3]{2,1,0:T(8,128)(2,1)S(1)}, u32[]{:S(2)}, u32[]{:S(2)}) collective-permute-start(bf16[20,32,3]{2,1,0:T(8,128)(2,1)S(1)} %get-tuple-element.29), channel_id=1, source_target_pairs={{0,1},{1,2},{2,3},{4,5},{5,6},{6,7},{8,9},{9,10},{10,11},{12,13},{... | collective-permute-start | bytes 11528 | tf_op jit(solution)/shard_map/ppermute | solution.py:17
  11.4 7.4 %collective-permute-start.2 = (bf16[20,32,3]{2,1,0:T(8,128)(2,1)S(1)}, bf16[20,32,3]{2,1,0:T(8,128)(2,1)S(1)}, u32[]{:S(2)}, u32[]{:S(2)}) collective-permute-start(bf16[20,32,3]{2,1,0:T(8,128)(2,1)S(1)} %get-tuple-element.30), channel_id=1, source_target_pairs={{1,0},{2,1},{3,2},{5,4},{6,5},{7,6},{9,8},{10,9},{11,10},{13,12},{... | collective-permute-start | bytes 11528 | tf_op jit(solution)/shard_map/ppermute | solution.py:17
  14.8 0.7 %copy-start.2 = (bf16[2,3,16,16]{3,2,1,0:T(8,128)(2,1)S(1)}, bf16[2,3,16,16]{3,2,1,0:T(8,128)(2,1)}, u32[]{:S(2)}) copy-start(bf16[2,3,16,16]{3,2,1,0:T(8,128)(2,1)} %param.16) | copy-start | bytes 9220
  15.7 0.7 %copy-start.4 = (f32[2,16]{1,0:T(2,128)S(1)}, f32[2,16]{1,0:T(2,128)}, u32[]{:S(2)}) copy-start(f32[2,16]{1,0:T(2,128)} %param.17) | copy-start | bytes 388
  16.4 0.7 %copy-start.5 = (f32[16]{0:T(128)S(1)}, f32[16]{0:T(128)}, u32[]{:S(2)}) copy-start(f32[16]{0:T(128)} %param.14) | copy-start | bytes 196
  17.2 0.7 %copy-start.6 = (f32[16]{0:T(128)S(1)}, f32[16]{0:T(128)}, u32[]{:S(2)}) copy-start(f32[16]{0:T(128)} %param.18) | copy-start | bytes 196

commit v2 on v1

--- a/solution.py
+++ b/solution.py
@@ -106,12 +106,20 @@
 
         lax.fori_loop(0, n_in, stem, 0)
 
-        def spatial(block, src_ref, n, lo, hi):
+        def spatial(block, src_ref, n, wide, lo, hi):
+            lo_y, hi_y = wide
+            width_y = hi_y - lo_y
+            dx_shifts = [(-(base + dx - 1)) % total for dx in range(3)]
+
             def body(f, carry):
                 x = src_ref[f]
-                pieces = [pltpu.roll(x, sh, 1)[:, lo:hi] if sh else x[:, lo:hi] for sh in shifts]
+                pieces = [pltpu.roll(x, sh, 1)[:, lo_y:hi_y] for sh in dx_shifts]
                 patches = jnp.concatenate(pieces, axis=0)
-                acc = jnp.dot(wsp_ref[block], patches, preferred_element_type=jnp.float32)
+                y = jnp.dot(wsp_ref[block], patches, preferred_element_type=jnp.float32)
+                a, b = lo - lo_y, hi - lo_y
+                up = pltpu.roll(y[0:channels], pitch, 1)[:, a:b]
+                down = pltpu.roll(y[2 * channels:3 * channels], width_y - pitch, 1)[:, a:b]
+                acc = up + y[channels:2 * channels, a:b] + down
                 s_ref[f, :, lo:hi] = acc.astype(jnp.bfloat16)
                 return carry
             lax.fori_loop(0, n, body, 0)
@@ -123,7 +131,7 @@
             return (centre + jnp.maximum(acc, 0.0)).astype(jnp.bfloat16)
 
         lo1, hi1 = spans[1]
-        spatial(0, ha_ref, n_in, lo1, hi1)
+        spatial(0, ha_ref, n_in, spans[0], lo1, hi1)
         mask1 = mask_ref[1, :, lo1:hi1] > 0.5
 
         def block0(k, carry):
@@ -134,7 +142,7 @@
 
         lax.fori_loop(0, n_in - 2, block0, 0)
         lo2, hi2 = spans[2]
-        spatial(1, hb2_ref, n_in - 2, lo2, hi2)
+        spatial(1, hb2_ref, n_in - 2, spans[1], lo2, hi2)
 
         def block1(k, carry):
             h2 = temporal(1, hb2_ref, k, lo2, hi2).astype(jnp.float32)
@@ -168,7 +176,8 @@
     wst = jnp.zeros((channels, 32), jnp.bfloat16)
     wst = wst.at[:, 0:9].set(w_hi.T).at[:, 16:25].set(w_lo.T)
     bst = stem_bias.astype(jnp.float32)[:, None]
-    wsp = spatial_weight.transpose(0, 2, 1, 3).reshape(2, channels, 9 * channels)
+    wsp = spatial_weight.reshape(2, 3, 3, channels, channels).transpose(0, 1, 3, 2, 4)
+    wsp = wsp.reshape(2, 3 * channels, 3 * channels)
     tw = temporal_weight.transpose(0, 2, 1, 3).reshape(2, channels, 3 * channels)
     tb = temporal_bias.astype(jnp.float32)[:, :, None]
     hw = head_weight.astype(jnp.float32)[:, None]

time: 56.6 us -> 54.4 us (0.961)
  Pallas kernels: 34.1 us -> 31.9 us
    pallas_call x1, Pallas kernels: 34.1 us -> 31.9 us  [shards(): pl.pallas_call(make_kernel(n_in, count, pitch, length, base, total, heigh...]
where the time goes in v2:
time: 54.4 us; the launch traced here: 54 us
  Pallas kernels  31.9 us (59%)
  starting transfers between devices  9.97 us (18%)
  local copies, waits for them, and re-layouts  7.71 us (14%)
  other arithmetic  3.48 us (6%)
  between operations  0.88 us (2%)
    pallas_call x1, Pallas kernels, shards(): pl.pallas_call(make_kernel(n_in, count, pitch, length, base, total, heigh...  31.9 us
    ppermute x3, starting transfers between devices, shifted(): lax.ppermute(value, axis, [(source, source + steps) for source in range(l...  9.97 us
    unnamed x15, local copies, waits for them, and re-layouts  3.32 us
    another operation x3, other arithmetic  2.56 us
  transfers between devices with their start and end apart: 3, of which 0 were waited for; matrix products, arithmetic and copies ran while one was open for 7% of the time, Pallas kernels for 0%

profile of v2, /device:TPU:1, one launch (start us, length us, event | category | flops | bytes accessed | tf_op | source)
XLA Modules:
  0.0 54.0 jit_solution(1629262148953516912)
XLA Ops:
  0.0 0.0 copy-start
  0.0 0.8 %slice_bitcast_fusion.1 = bf16[4,32,128]{2,1,0:T(8,128)(2,1)S(1)} fusion(bf16[16,1,32,128]{3,2,0,1:T(8,128)(2,1)} %bitcast.23), kind=kLoop, calls=%fused_computation.17 | loop fusion | bytes 65536 | tf_op jit(solution)/shard_map/slice | solution.py:161
  0.8 3.9 %collective-permute-start = (bf16[4,32,128]{2,1,0:T(8,128)(2,1)S(1)}, bf16[4,32,128]{2,1,0:T(8,128)(2,1)S(1)}, u32[]{:S(2)}, u32[]{:S(2)}) collective-permute-start(bf16[4,32,128]{2,1,0:T(8,128)(2,1)S(1)} %slice_bitcast_fusion.1), channel_id=1, source_target_pairs={{0,4},{4,8},{8,12},{12,16},{16,20},{20,24},{24,28},{1,5},{5,9},{9,... | collective-permute-start | bytes 98312 | tf_op jit(solution)/shard_map/ppermute | solution.py:17
  4.8 0.3 compare_and_fusion
  5.1 0.0 copy-start.3
  5.1 0.1 add_convert_fusion
  5.2 0.6 %copy-done.3 = f32[9,16]{1,0:T(8,128)S(1)} copy-done((f32[9,16]{1,0:T(8,128)S(1)}, f32[9,16]{1,0:T(8,128)}, u32[]{:S(2)}) %copy-start.3) | copy-done | bytes 600
  5.8 0.1 copy.18
  5.9 0.6 %compare_reduce_fusion.1 = pred[]{:T(512)} fusion(), kind=kLoop, calls=%fused_computation.25 | loop fusion | flops 5 | bytes 1 | tf_op jit(solution)/shard_map/reduce.2
  6.5 0.6 %compare_reduce_fusion = pred[]{:T(512)} fusion(), kind=kLoop, calls=%fused_computation.24 | loop fusion | flops 7 | bytes 1 | tf_op jit(solution)/shard_map/reduce.3
  7.2 0.0 collective-permute-done
  7.2 0.0 copy-done
  7.2 0.1 maximum_select_fusion
  7.3 0.0 copy-start.1
  7.3 4.1 %collective-permute-start.1 = (bf16[20,32,3]{2,1,0:T(8,128)(2,1)S(1)}, bf16[20,32,3]{2,1,0:T(8,128)(2,1)S(1)}, u32[]{:S(2)}, u32[]{:S(2)}) collective-permute-start(bf16[20,32,3]{2,1,0:T(8,128)(2,1)S(1)} %get-tuple-element.29), channel_id=1, source_target_pairs={{0,1},{1,2},{2,3},{4,5},{5,6},{6,7},{8,9},{9,10},{10,11},{12,13},{... | collective-permute-start | bytes 11528 | tf_op jit(solution)/shard_map/ppermute | solution.py:17
  11.4 1.9 %collective-permute-start.2 = (bf16[20,32,3]{2,1,0:T(8,128)(2,1)S(1)}, bf16[20,32,3]{2,1,0:T(8,128)(2,1)S(1)}, u32[]{:S(2)}, u32[]{:S(2)}) collective-permute-start(bf16[20,32,3]{2,1,0:T(8,128)(2,1)S(1)} %get-tuple-element.30), channel_id=1, source_target_pairs={{1,0},{2,1},{3,2},{5,4},{6,5},{7,6},{9,8},{10,9},{11,10},{13,12},{... | collective-permute-start | bytes 11528 | tf_op jit(solution)/shard_map/ppermute | solution.py:17
  13.4 1.3 %fusion.4 = (bf16[16,9]{1,0:T(8,128)(2,1)S(1)}, bf16[16,9]{1,0:T(8,128)(2,1)S(1)}) fusion(f32[9,16]{0,1:T(8,128)S(1)} %copy.18, pred[]{:T(512)} %compare_reduce_fusion, pred[]{:T(512)} %compare_reduce_fusion.1), kind=kLoop, calls=%fused_computation.22 | loop fusion | flops 864 | bytes 1154 | tf_op jit(solution)/shard_map/transpose.19
  14.7 0.0 copy-done.1
  14.7 0.0 copy-start.2
  14.8 0.1 reshape.213.wsp_ref
  14.9 0.6 %copy-done.2 = bf16[2,3,16,16]{3,2,1,0:T(8,128)(2,1)S(1)} copy-done((bf16[2,3,16,16]{3,2,1,0:T(8,128)(2,1)S(1)}, bf16[2,3,16,16]{3,2,1,0:T(8,128)(2,1)}, u32[]{:S(2)}) %copy-start.2) | copy-done | bytes 3096
  15.5 0.1 reshape.214.tw_ref
  15.6 0.0 copy-start.4
  15.6 0.7 %copy-done.4 = f32[2,16]{1,0:T(2,128)S(1)} copy-done((f32[2,16]{1,0:T(2,128)S(1)}, f32[2,16]{1,0:T(2,128)}, u32[]{:S(2)}) %copy-start.4) | copy-done | bytes 152
  16.3 0.1 copy.23.tb_ref
  16.4 0.0 copy-start.5
  16.4 0.7 %copy-done.5 = f32[16]{0:T(128)S(1)} copy-done((f32[16]{0:T(128)S(1)}, f32[16]{0:T(128)}, u32[]{:S(2)}) %copy-start.5) | copy-done | bytes 88
  17.0 0.1 copy.22.bst_ref
  17.1 0.0 copy-start.6
  17.1 0.7 %copy-done.6 = f32[16]{0:T(128)S(1)} copy-done((f32[16]{0:T(128)S(1)}, f32[16]{0:T(128)}, u32[]{:S(2)}) %copy-start.6) | copy-done | bytes 88
  17.8 0.1 copy.24.hw_ref
  18.5 0.2 scatter.9.wst_ref
  18.8 0.0 collective-permute-done.1
  18.8 0.0 collective-permute-done.2
  18.8 0.4 pad_maximum_fusion
  19.2 0.4 convert_element_type.31
  19.7 0.3 reshape.216.vp_ref
  20.0 31.9 %shard_map.82 = f32[16,1,5120]{2,1,0:T(1,128)S(1)} custom-call(s32[1]{0:T(128)} %bitcast.first_ref, f32[20,1,5632]{2,1,0:T(1,128)S(1)} %reshape.216.vp_ref, f32[2,1,5120]{2,1,0:T(1,128)S(1)} %reshape.217.mask_ref, bf16[16,32]{1,0:T(8,128)(2,1)S(1)} %scatter.9.wst_ref, f32[16,1]{1,0:T(8,128)S(1)} %copy.22.bst_ref, bf16[2,48,48]{2,1,0:T(8,128)(2,1)S(1)} %reshape.213.wsp_ref, ...), custom_call_target="tpu_custom_call" | custom-call | tf_op jit(solution)/shard_map/pallas_call | solution.py:191
  51.9 0.8 %slice_reduce_fusion = f32[16,5092]{1,0:T(8,128)S(1)} fusion(f32[16,1,5120]{2,1,0:T(1,128)S(1)} %shard_map.82), kind=kLoop, calls=%fused_computation.1 | loop fusion | bytes 651776 | tf_op jit(solution)/shard_map/slice | solution.py:203
  52.8 0.4 reshape_squeeze.3
  53.1 0.8 %slice_bitcast_fusion = f32[16,1,32,128]{3,2,1,0:T(8,128)} fusion(f32[16,38,134]{2,1,0:T(8,128)S(1)} %reshape_squeeze.3), kind=kLoop, calls=%fused_computation.3 | loop fusion | bytes 524288 | tf_op jit(solution)/shard_map/broadcast_in_dim | solution.py:205
  (6 shorter events, 0.1 us)
Async XLA Ops:
  0.0 7.2 %copy-start = (bf16[16,1,32,128]{3,2,1,0:T(8,128)(2,1)S(1)}, bf16[16,1,32,128]{3,2,1,0:T(8,128)(2,1)}, u32[]{:S(2)}) copy-start(bf16[16,1,32,128]{3,2,1,0:T(8,128)(2,1)} %param.12) | copy-start | bytes 393220
  0.8 6.3 %collective-permute-start = (bf16[4,32,128]{2,1,0:T(8,128)(2,1)S(1)}, bf16[4,32,128]{2,1,0:T(8,128)(2,1)S(1)}, u32[]{:S(2)}, u32[]{:S(2)}) collective-permute-start(bf16[4,32,128]{2,1,0:T(8,128)(2,1)S(1)} %slice_bitcast_fusion.1), channel_id=1, source_target_pairs={{0,4},{4,8},{8,12},{12,16},{16,20},{20,24},{24,28},{1,5},{5,9},{9,... | collective-permute-start | bytes 98312 | tf_op jit(solution)/shard_map/ppermute | solution.py:17
  5.1 0.7 %copy-start.3 = (f32[9,16]{1,0:T(8,128)S(1)}, f32[9,16]{1,0:T(8,128)}, u32[]{:S(2)}) copy-start(f32[9,16]{1,0:T(8,128)} %param.13) | copy-start | bytes 1732
  7.3 7.4 %copy-start.1 = (bf16[2,9,16,16]{3,2,1,0:T(8,128)(2,1)S(1)}, bf16[2,9,16,16]{3,2,1,0:T(8,128)(2,1)}, u32[]{:S(2)}) copy-start(bf16[2,9,16,16]{3,2,1,0:T(8,128)(2,1)} %param.15) | copy-start | bytes 27652
  7.3 11.4 %collective-permute-start.1 = (bf16[20,32,3]{2,1,0:T(8,128)(2,1)S(1)}, bf16[20,32,3]{2,1,0:T(8,128)(2,1)S(1)}, u32[]{:S(2)}, u32[]{:S(2)}) collective-permute-start(bf16[20,32,3]{2,1,0:T(8,128)(2,1)S(1)} %get-tuple-element.29), channel_id=1, source_target_pairs={{0,1},{1,2},{2,3},{4,5},{5,6},{6,7},{8,9},{9,10},{10,11},{12,13},{... | collective-permute-start | bytes 11528 | tf_op jit(solution)/shard_map/ppermute | solution.py:17
  11.4 7.3 %collective-permute-start.2 = (bf16[20,32,3]{2,1,0:T(8,128)(2,1)S(1)}, bf16[20,32,3]{2,1,0:T(8,128)(2,1)S(1)}, u32[]{:S(2)}, u32[]{:S(2)}) collective-permute-start(bf16[20,32,3]{2,1,0:T(8,128)(2,1)S(1)} %get-tuple-element.30), channel_id=1, source_target_pairs={{1,0},{2,1},{3,2},{5,4},{6,5},{7,6},{9,8},{10,9},{11,10},{13,12},{... | collective-permute-start | bytes 11528 | tf_op jit(solution)/shard_map/ppermute | solution.py:17
  14.7 0.7 %copy-start.2 = (bf16[2,3,16,16]{3,2,1,0:T(8,128)(2,1)S(1)}, bf16[2,3,16,16]{3,2,1,0:T(8,128)(2,1)}, u32[]{:S(2)}) copy-start(bf16[2,3,16,16]{3,2,1,0:T(8,128)(2,1)} %param.16) | copy-start | bytes 9220
  15.6 0.7 %copy-start.4 = (f32[2,16]{1,0:T(2,128)S(1)}, f32[2,16]{1,0:T(2,128)}, u32[]{:S(2)}) copy-start(f32[2,16]{1,0:T(2,128)} %param.17) | copy-start | bytes 388
  16.4 0.7 %copy-start.5 = (f32[16]{0:T(128)S(1)}, f32[16]{0:T(128)}, u32[]{:S(2)}) copy-start(f32[16]{0:T(128)} %param.14) | copy-start | bytes 196
  17.1 0.7 %copy-start.6 = (f32[16]{0:T(128)S(1)}, f32[16]{0:T(128)}, u32[]{:S(2)}) copy-start(f32[16]{0:T(128)} %param.18) | copy-start | bytes 196

commit v3 on v2

--- a/solution.py
+++ b/solution.py
@@ -91,20 +91,22 @@
 
         lo0, hi0 = spans[0]
         mask0 = mask_ref[0, :, lo0:hi0] > 0.5
-        filler = jnp.zeros((16 - len(shifts), hi0 - lo0), jnp.float32)
-
-        def stem(f, carry):
-            v = vp_ref[f]
+        group = 8
+        filler = jnp.zeros((group, hi0 - lo0), jnp.float32)
+        for g in range(vp_ref.shape[0] // group):
+            v = vp_ref[g * group:(g + 1) * group, :]
             rows = [pltpu.roll(v, sh, 1)[:, lo0:hi0] if sh else v[:, lo0:hi0] for sh in shifts]
             patch = jnp.concatenate(rows + [filler], axis=0).astype(jnp.bfloat16)
             patch = jnp.concatenate([patch, patch], axis=0)
             acc = jnp.dot(wst_ref[...], patch, preferred_element_type=jnp.float32)
-            h0 = jnp.maximum(acc + bst_ref[...], 0.0).astype(jnp.bfloat16)
-            keep = mask0 & (first + f >= 0)
-            ha_ref[f, :, base + lo0:base + hi0] = jnp.where(keep, h0, jnp.zeros_like(h0))
-            return carry
-
-        lax.fori_loop(0, n_in, stem, 0)
+            for j in range(group):
+                f = g * group + j
+                if f >= n_in:
+                    break
+                part = acc[j * channels:(j + 1) * channels]
+                h0 = jnp.maximum(part + bst_ref[...], 0.0).astype(jnp.bfloat16)
+                keep = mask0 & (first + f >= 0)
+                ha_ref[f, :, base + lo0:base + hi0] = jnp.where(keep, h0, jnp.zeros_like(h0))
 
         def spatial(block, src_ref, n, wide, lo, hi):
             lo_y, hi_y = wide
@@ -167,14 +169,20 @@
     base = round_up(pitch + 1, 128)
     total = length + 2 * base
     flat = extended.reshape(n_in, rows * pitch)
-    flat = jnp.pad(flat.astype(jnp.float32), ((0, 0), (base, total - base - rows * pitch)))
-    vp = flat[:, None, :]
+    n_pad = round_up(n_in, 8)
+    flat = jnp.pad(flat.astype(jnp.float32), ((0, n_pad - n_in), (base, total - base - rows * pitch)))
+    vp = flat
 
     channels = stem_weight.shape[1]
-    w_hi = stem_weight.astype(jnp.bfloat16)
-    w_lo = (stem_weight - w_hi.astype(jnp.float32)).astype(jnp.bfloat16)
-    wst = jnp.zeros((channels, 32), jnp.bfloat16)
-    wst = wst.at[:, 0:9].set(w_hi.T).at[:, 16:25].set(w_lo.T)
+    w_hi = stem_weight.astype(jnp.bfloat16).astype(jnp.float32)
+    w_lo = stem_weight - w_hi
+    eye = jnp.eye(8, dtype=jnp.float32)
+
+    def spread_taps(w):
+        w = jnp.pad(w, ((0, 1), (0, 0)))
+        return jnp.einsum("to,jk->jotk", w, eye).reshape(8 * channels, 8 * w.shape[0])
+
+    wst = jnp.concatenate([spread_taps(w_hi), spread_taps(w_lo)], axis=1).astype(jnp.bfloat16)
     bst = stem_bias.astype(jnp.float32)[:, None]
     wsp = spatial_weight.reshape(2, 3, 3, channels, channels).transpose(0, 1, 3, 2, 4)
     wsp = wsp.reshape(2, 3 * channels, 3 * channels)

time: 54.4 us -> 48.2 us (0.89)
  Pallas kernels: 31.9 us -> 26.9 us
  other arithmetic: 3.48 us -> 1.16 us
  waiting for transfers between devices: 0.01 us -> 1.89 us
  local copies, waits for them, and re-layouts: 7.71 us -> 7.03 us
    pallas_call x1, Pallas kernels: 31.9 us -> 26.9 us  [shards(): pl.pallas_call(make_kernel(n_in, count, pitch, length, base, total, heigh...]
    another operation x3 -> x1, other arithmetic: 2.56 us -> 0.01 us
    ppermute x3, waiting for transfers between devices: 0.01 us -> 1.89 us  [shifted(): lax.ppermute(value, axis, [(source, source + steps) for source in range(l...]
    unnamed x15 -> x14, local copies, waits for them, and re-layouts: 3.32 us -> 2.75 us
  transfers between devices with their start and end apart: 3 -> 3, of which waited for: 0 -> 1; matrix products, arithmetic and copies ran while one was open for 7% -> 3% of each run, Pallas kernels for 0% -> 0%
where the time goes in v3:
time: 48.2 us; the launch traced here: 47.7 us
  Pallas kernels  26.9 us (56%)
  starting transfers between devices  9.84 us (20%)
  local copies, waits for them, and re-layouts  7.03 us (15%)
  waiting for transfers between devices  1.89 us (4%)
  other arithmetic  1.16 us (2%)
  between operations  0.94 us (2%)
    pallas_call x1, Pallas kernels, shards(): pl.pallas_call(make_kernel(n_in, count, pitch, length, base, total, heigh...  26.9 us
    ppermute x3, starting transfers between devices, shifted(): lax.ppermute(value, axis, [(source, source + steps) for source in range(l...  9.84 us
    unnamed x14, local copies, waits for them, and re-layouts  2.75 us
    ppermute x3, waiting for transfers between devices, shifted(): lax.ppermute(value, axis, [(source, source + steps) for source in range(l...  1.89 us
  transfers between devices with their start and end apart: 3, of which 1 were waited for; matrix products, arithmetic and copies ran while one was open for 3% of the time, Pallas kernels for 0%

profile of v3, /device:TPU:1, one launch (start us, length us, event | category | flops | bytes accessed | tf_op | source)
XLA Modules:
  0.0 47.7 jit_solution(15481113233818302518)
XLA Ops:
  0.0 0.8 %slice_bitcast_fusion.1 = bf16[4,32,128]{2,1,0:T(8,128)(2,1)S(1)} fusion(bf16[16,1,32,128]{3,2,0,1:T(8,128)(2,1)} %bitcast.31), kind=kLoop, calls=%fused_computation.22 | loop fusion | bytes 65536 | tf_op jit(solution)/shard_map/slice | solution.py:163
  0.8 3.9 %collective-permute-start = (bf16[4,32,128]{2,1,0:T(8,128)(2,1)S(1)}, bf16[4,32,128]{2,1,0:T(8,128)(2,1)S(1)}, u32[]{:S(2)}, u32[]{:S(2)}) collective-permute-start(bf16[4,32,128]{2,1,0:T(8,128)(2,1)S(1)} %slice_bitcast_fusion.1), channel_id=1, source_target_pairs={{0,4},{4,8},{8,12},{12,16},{16,20},{20,24},{24,28},{1,5},{5,9},{9,... | collective-permute-start | bytes 98312 | tf_op jit(solution)/shard_map/ppermute | solution.py:17
  4.7 0.0 copy-start.3
  4.8 0.7 %copy-done.3 = f32[9,16]{1,0:T(8,128)S(1)} copy-done((f32[9,16]{1,0:T(8,128)S(1)}, f32[9,16]{1,0:T(8,128)}, u32[]{:S(2)}) %copy-start.3) | copy-done | bytes 600
  5.5 0.3 compare_and_fusion
  5.8 0.1 add_convert_fusion
  5.8 0.1 fusion
  6.0 0.1 reshape.171
  6.1 0.1 copy.18
  6.2 0.0 copy-start
  6.3 0.1 reshape.172
  6.4 0.1 copy.19
  6.5 0.0 collective-permute-done
  6.5 0.6 %copy-done = bf16[16,1,32,128]{3,2,1,0:T(8,128)(2,1)S(1)} copy-done((bf16[16,1,32,128]{3,2,1,0:T(8,128)(2,1)S(1)}, bf16[16,1,32,128]{3,2,1,0:T(8,128)(2,1)}, u32[]{:S(2)}) %copy-start) | copy-done | bytes 131096
  7.2 0.1 maximum_select_fusion
  7.3 4.0 %collective-permute-start.1 = (bf16[20,32,3]{2,1,0:T(8,128)(2,1)S(1)}, bf16[20,32,3]{2,1,0:T(8,128)(2,1)S(1)}, u32[]{:S(2)}, u32[]{:S(2)}) collective-permute-start(bf16[20,32,3]{2,1,0:T(8,128)(2,1)S(1)} %get-tuple-element.5), channel_id=1, source_target_pairs={{0,1},{1,2},{2,3},{4,5},{5,6},{6,7},{8,9},{9,10},{10,11},{12,13},{... | collective-permute-start | bytes 11528 | tf_op jit(solution)/shard_map/ppermute | solution.py:17
  11.3 1.9 %collective-permute-start.2 = (bf16[20,32,3]{2,1,0:T(8,128)(2,1)S(1)}, bf16[20,32,3]{2,1,0:T(8,128)(2,1)S(1)}, u32[]{:S(2)}, u32[]{:S(2)}) collective-permute-start(bf16[20,32,3]{2,1,0:T(8,128)(2,1)S(1)} %get-tuple-element.6), channel_id=1, source_target_pairs={{1,0},{2,1},{3,2},{5,4},{6,5},{7,6},{9,8},{10,9},{11,10},{13,12},{... | collective-permute-start | bytes 11528 | tf_op jit(solution)/shard_map/ppermute | solution.py:17
  13.2 0.0 copy-start.5
  13.2 0.1 pad_maximum_fusion.2.wst_ref
  13.3 0.0 copy-start.6
  13.3 0.0 copy-start.2
  14.0 0.0 copy-done.5
  14.0 0.1 copy.22.bst_ref
  14.1 0.0 copy-done.6
  14.1 0.1 copy.24.hw_ref
  14.2 0.0 copy-start.4
  14.2 0.7 %copy-done.4 = f32[2,16]{1,0:T(2,128)S(1)} copy-done((f32[2,16]{1,0:T(2,128)S(1)}, f32[2,16]{1,0:T(2,128)}, u32[]{:S(2)}) %copy-start.4) | copy-done | bytes 152
  14.9 0.1 copy.23.tb_ref
  15.0 0.0 copy-done.2
  15.0 0.0 copy-start.1
  15.0 0.1 reshape.175.tw_ref
  15.1 0.8 %copy-done.1 = bf16[2,9,16,16]{3,2,1,0:T(8,128)(2,1)S(1)} copy-done((bf16[2,9,16,16]{3,2,1,0:T(8,128)(2,1)S(1)}, bf16[2,9,16,16]{3,2,1,0:T(8,128)(2,1)}, u32[]{:S(2)}) %copy-start.1) | copy-done | bytes 9240
  15.9 0.1 reshape.174.wsp_ref
  16.0 0.0 collective-permute-done.1
  16.0 1.9 %collective-permute-done.2 = bf16[20,32,3]{2,1,0:T(8,128)(2,1)S(1)} collective-permute-done((bf16[20,32,3]{2,1,0:T(8,128)(2,1)S(1)}, bf16[20,32,3]{2,1,0:T(8,128)(2,1)S(1)}, u32[]{:S(2)}, u32[]{:S(2)}) %collective-permute-start.2) | collective-permute-done | bytes 3872 | tf_op jit(solution)/shard_map/ppermute | solution.py:17
  17.9 0.4 pad_maximum_fusion
  18.4 0.4 convert_element_type.33
  18.8 26.9 %shard_map.82 = f32[16,1,5120]{2,1,0:T(1,128)S(1)} custom-call(s32[1]{0:T(128)} %bitcast.first_ref, f32[24,5632]{1,0:T(8,128)S(1)} %pad_convert_fusion.vp_ref, f32[2,1,5120]{2,1,0:T(1,128)S(1)} %reshape.177.mask_ref, bf16[128,160]{1,0:T(8,128)(2,1)S(1)} %pad_maximum_fusion.2.wst_ref, f32[16,1]{1,0:T(8,128)S(1)} %copy.22.bst_ref, ...), custom_call_target="tpu_custom_call" | custom-call | tf_op jit(solution)/shard_map/pallas_call | solution.py:199
  45.7 0.8 %slice_reduce_fusion = f32[16,5092]{1,0:T(8,128)S(1)} fusion(f32[16,1,5120]{2,1,0:T(1,128)S(1)} %shard_map.82), kind=kLoop, calls=%fused_computation.1 | loop fusion | bytes 651776 | tf_op jit(solution)/shard_map/slice | solution.py:211
  46.5 0.4 reshape_squeeze.3
  46.9 0.8 %slice_bitcast_fusion = f32[16,1,32,128]{3,2,1,0:T(8,128)} fusion(f32[16,38,134]{2,1,0:T(8,128)S(1)} %reshape_squeeze.3), kind=kLoop, calls=%fused_computation.5 | loop fusion | bytes 524288 | tf_op jit(solution)/shard_map/broadcast_in_dim | solution.py:213
  (9 shorter events, 0.2 us)
Async XLA Ops:
  0.8 5.8 %collective-permute-start = (bf16[4,32,128]{2,1,0:T(8,128)(2,1)S(1)}, bf16[4,32,128]{2,1,0:T(8,128)(2,1)S(1)}, u32[]{:S(2)}, u32[]{:S(2)}) collective-permute-start(bf16[4,32,128]{2,1,0:T(8,128)(2,1)S(1)} %slice_bitcast_fusion.1), channel_id=1, source_target_pairs={{0,4},{4,8},{8,12},{12,16},{16,20},{20,24},{24,28},{1,5},{5,9},{9,... | collective-permute-start | bytes 98312 | tf_op jit(solution)/shard_map/ppermute | solution.py:17
  4.7 0.7 %copy-start.3 = (f32[9,16]{1,0:T(8,128)S(1)}, f32[9,16]{1,0:T(8,128)}, u32[]{:S(2)}) copy-start(f32[9,16]{1,0:T(8,128)} %param.9) | copy-start | bytes 1732
  6.2 0.9 %copy-start = (bf16[16,1,32,128]{3,2,1,0:T(8,128)(2,1)S(1)}, bf16[16,1,32,128]{3,2,1,0:T(8,128)(2,1)}, u32[]{:S(2)}) copy-start(bf16[16,1,32,128]{3,2,1,0:T(8,128)(2,1)} %param.8) | copy-start | bytes 393220
  7.3 8.7 %collective-permute-start.1 = (bf16[20,32,3]{2,1,0:T(8,128)(2,1)S(1)}, bf16[20,32,3]{2,1,0:T(8,128)(2,1)S(1)}, u32[]{:S(2)}, u32[]{:S(2)}) collective-permute-start(bf16[20,32,3]{2,1,0:T(8,128)(2,1)S(1)} %get-tuple-element.5), channel_id=1, source_target_pairs={{0,1},{1,2},{2,3},{4,5},{5,6},{6,7},{8,9},{9,10},{10,11},{12,13},{... | collective-permute-start | bytes 11528 | tf_op jit(solution)/shard_map/ppermute | solution.py:17
  11.3 6.6 %collective-permute-start.2 = (bf16[20,32,3]{2,1,0:T(8,128)(2,1)S(1)}, bf16[20,32,3]{2,1,0:T(8,128)(2,1)S(1)}, u32[]{:S(2)}, u32[]{:S(2)}) collective-permute-start(bf16[20,32,3]{2,1,0:T(8,128)(2,1)S(1)} %get-tuple-element.6), channel_id=1, source_target_pairs={{1,0},{2,1},{3,2},{5,4},{6,5},{7,6},{9,8},{10,9},{11,10},{13,12},{... | collective-permute-start | bytes 11528 | tf_op jit(solution)/shard_map/ppermute | solution.py:17
  13.2 0.8 %copy-start.5 = (f32[16]{0:T(128)S(1)}, f32[16]{0:T(128)}, u32[]{:S(2)}) copy-start(f32[16]{0:T(128)} %param.10) | copy-start | bytes 196
  13.3 0.8 %copy-start.6 = (f32[16]{0:T(128)S(1)}, f32[16]{0:T(128)}, u32[]{:S(2)}) copy-start(f32[16]{0:T(128)} %param.14) | copy-start | bytes 196
  13.3 1.6 %copy-start.2 = (bf16[2,3,16,16]{3,2,1,0:T(8,128)(2,1)S(1)}, bf16[2,3,16,16]{3,2,1,0:T(8,128)(2,1)}, u32[]{:S(2)}) copy-start(bf16[2,3,16,16]{3,2,1,0:T(8,128)(2,1)} %param.12) | copy-start | bytes 9220
  14.2 0.7 %copy-start.4 = (f32[2,16]{1,0:T(2,128)S(1)}, f32[2,16]{1,0:T(2,128)}, u32[]{:S(2)}) copy-start(f32[2,16]{1,0:T(2,128)} %param.13) | copy-start | bytes 388
  15.0 0.9 %copy-start.1 = (bf16[2,9,16,16]{3,2,1,0:T(8,128)(2,1)S(1)}, bf16[2,9,16,16]{3,2,1,0:T(8,128)(2,1)}, u32[]{:S(2)}) copy-start(bf16[2,9,16,16]{3,2,1,0:T(8,128)(2,1)} %param.11) | copy-start | bytes 27652

commit v4 on v3

--- a/solution.py
+++ b/solution.py
@@ -126,33 +126,34 @@
                 return carry
             lax.fori_loop(0, n, body, 0)
 
-        def temporal(block, src_ref, k, lo, hi):
-            stacked = jnp.concatenate([s_ref[k, :, lo:hi], s_ref[k + 1, :, lo:hi], s_ref[k + 2, :, lo:hi]], axis=0)
-            acc = jnp.dot(tw_ref[block], stacked, preferred_element_type=jnp.float32) + tb_ref[block]
-            centre = src_ref[k + 2, :, base + lo:base + hi].astype(jnp.float32)
-            return (centre + jnp.maximum(acc, 0.0)).astype(jnp.bfloat16)
-
+        def temporal(block, src_ref, n_out, lo, hi, finish):
+            for k0 in range(0, n_out, group):
+                stacked = jnp.concatenate([s_ref[k0 + jj, :, lo:hi] for jj in range(group + 2)], axis=0)
+                acc = jnp.dot(tw_ref[block], stacked, preferred_element_type=jnp.float32)
+                for j in range(min(group, n_out - k0)):
+                    k = k0 + j
+                    part = acc[j * channels:(j + 1) * channels] + tb_ref[block]
+                    centre = src_ref[k + 2, :, base + lo:base + hi].astype(jnp.float32)
+                    finish(k, (centre + jnp.maximum(part, 0.0)).astype(jnp.bfloat16))
+
+        s_ref[n_in:, :, :] = jnp.zeros((s_ref.shape[0] - n_in, channels, length), jnp.bfloat16)
         lo1, hi1 = spans[1]
         spatial(0, ha_ref, n_in, spans[0], lo1, hi1)
         mask1 = mask_ref[1, :, lo1:hi1] > 0.5
 
-        def block0(k, carry):
-            h1 = temporal(0, ha_ref, k, lo1, hi1)
+        def finish0(k, h1):
             keep = mask1 & (first + 2 + k >= 0)
             hb2_ref[k, :, base + lo1:base + hi1] = jnp.where(keep, h1, jnp.zeros_like(h1))
-            return carry
-
-        lax.fori_loop(0, n_in - 2, block0, 0)
+
+        temporal(0, ha_ref, n_in - 2, lo1, hi1, finish0)
         lo2, hi2 = spans[2]
         spatial(1, hb2_ref, n_in - 2, spans[1], lo2, hi2)
 
-        def block1(k, carry):
-            h2 = temporal(1, hb2_ref, k, lo2, hi2).astype(jnp.float32)
-            head = jnp.sum(hw_ref[...] * h2, axis=0, keepdims=True) + hb_ref[...]
+        def finish1(k, h2):
+            head = jnp.sum(hw_ref[...] * h2.astype(jnp.float32), axis=0, keepdims=True) + hb_ref[...]
             out_ref[k, :, lo2:hi2] = head
-            return carry
-
-        lax.fori_loop(0, count, block1, 0)
+
+        temporal(1, hb2_ref, count, lo2, hi2, finish1)
 
     return kernel
 
@@ -186,7 +187,9 @@
     bst = stem_bias.astype(jnp.float32)[:, None]
     wsp = spatial_weight.reshape(2, 3, 3, channels, channels).transpose(0, 1, 3, 2, 4)
     wsp = wsp.reshape(2, 3 * channels, 3 * channels)
-    tw = temporal_weight.transpose(0, 2, 1, 3).reshape(2, channels, 3 * channels)
+    band = jnp.stack([jnp.eye(8, 10, d, dtype=jnp.float32) for d in range(3)])
+    tw = jnp.einsum("dja,bdoi->bjoai", band, temporal_weight.astype(jnp.float32))
+    tw = tw.reshape(2, 8 * channels, 10 * channels).astype(jnp.bfloat16)
     tb = temporal_bias.astype(jnp.float32)[:, :, None]
     hw = head_weight.astype(jnp.float32)[:, None]
     hb = head_bias.astype(jnp.float32).reshape(1, 1)
@@ -204,7 +207,7 @@
         scratch_shapes=[
             pltpu.VMEM((n_in, channels, total), jnp.bfloat16),
             pltpu.VMEM((n_in - 2, channels, total), jnp.bfloat16),
-            pltpu.VMEM((n_in, channels, length), jnp.bfloat16),
+            pltpu.VMEM((round_up(n_in - 2, 8) + 2, channels, length), jnp.bfloat16),
         ],
         compiler_params=pltpu.CompilerParams(vmem_limit_bytes=48 * 1024 * 1024),
     )(first, vp, masks, wst, bst, wsp, tw, tb, hw, hb)

time: 48.2 us -> 45.6 us (0.946)
  Pallas kernels: 26.9 us -> 23.5 us
  local copies, waits for them, and re-layouts: 7.03 us -> 5.7 us
  matrix products: 0 us -> 1.27 us
  other arithmetic: 1.16 us -> 2.02 us
    pallas_call x1, Pallas kernels: 26.9 us -> 23.5 us  [shards(): pl.pallas_call(make_kernel(n_in, count, pitch, length, base, total, heigh...]
    unnamed x14 -> x10, local copies, waits for them, and re-layouts: 2.75 us -> 0.03 us
    convert_element_type x0 -> x3, local copies, waits for them, and re-layouts: none -> 1.49 us  [shards(): tw = tw.reshape(2, 8 * channels, 10 * channels).astype(jnp.bfloat16)]
    dot_general x0 -> x1, matrix products: none -> 1.27 us  [shards(): jnp.einsum('dja,bdoi->bjoai', band, temporal_weight.astype(jnp.float32))]
    convert_element_type x1, other arithmetic: 0.01 us -> 0.78 us  [shards(): w_hi = stem_weight.astype(jnp.bfloat16).astype(jnp.float32)]
  transfers between devices with their start and end apart: 3 -> 3, of which waited for: 1 -> 1; matrix products, arithmetic and copies ran while one was open for 3% -> 11% of each run, Pallas kernels for 0% -> 0%
where the time goes in v4:
time: 45.6 us; the launch traced here: 45.2 us
  Pallas kernels  23.5 us (52%)
  starting transfers between devices  9.84 us (22%)
  local copies, waits for them, and re-layouts  5.7 us (12%)
  other arithmetic  2.02 us (4%)
  waiting for transfers between devices  1.91 us (4%)
  matrix products  1.27 us (3%)
  between operations  1 us (2%)
    pallas_call x1, Pallas kernels, shards(): pl.pallas_call(make_kernel(n_in, count, pitch, length, base, total, heigh...  23.5 us
    ppermute x3, starting transfers between devices, shifted(): lax.ppermute(value, axis, [(source, source + steps) for source in range(l...  9.84 us
    ppermute x3, waiting for transfers between devices, shifted(): lax.ppermute(value, axis, [(source, source + steps) for source in range(l...  1.91 us
    convert_element_type x3, local copies, waits for them, and re-layouts, shards(): tw = tw.reshape(2, 8 * channels, 10 * channels).astype(jnp.bfloat16)  1.49 us
    dot_general x1, matrix products, shards(): jnp.einsum('dja,bdoi->bjoai', band, temporal_weight.astype(jnp.float32))  1.27 us
  transfers between devices with their start and end apart: 3, of which 1 were waited for; matrix products, arithmetic and copies ran while one was open for 11% of the time, Pallas kernels for 0%

profile of v4, /device:TPU:1, one launch (start us, length us, event | category | flops | bytes accessed | tf_op | source)
XLA Modules:
  0.0 45.2 jit_solution(9839798859134934276)
XLA Ops:
  0.0 0.8 %slice_bitcast_fusion.1 = bf16[4,32,128]{2,1,0:T(8,128)(2,1)S(1)} fusion(bf16[16,1,32,128]{3,2,0,1:T(8,128)(2,1)} %bitcast.44), kind=kLoop, calls=%fused_computation.24 | loop fusion | bytes 65536 | tf_op jit(solution)/shard_map/slice | solution.py:164
  0.8 3.9 %collective-permute-start = (bf16[4,32,128]{2,1,0:T(8,128)(2,1)S(1)}, bf16[4,32,128]{2,1,0:T(8,128)(2,1)S(1)}, u32[]{:S(2)}, u32[]{:S(2)}) collective-permute-start(bf16[4,32,128]{2,1,0:T(8,128)(2,1)S(1)} %slice_bitcast_fusion.1), channel_id=1, source_target_pairs={{0,4},{4,8},{8,12},{12,16},{16,20},{20,24},{24,28},{1,5},{5,9},{9,... | collective-permute-start | bytes 98312 | tf_op jit(solution)/shard_map/ppermute | solution.py:17
  4.8 0.8 %convert_convert_fusion = (f32[9,16]{1,0:T(8,128)S(1)}, f32[9,16]{1,0:T(8,128)S(1)}) fusion(f32[9,16]{1,0:T(8,128)} %param.9), kind=kLoop, calls=%fused_computation.37 | loop fusion | flops 432 | bytes 1728 | tf_op jit(solution)/shard_map/convert_element_type | solution.py:178
  5.6 0.0 copy-start
  5.6 0.3 compare_and_fusion
  5.9 0.1 add_convert_fusion
  6.0 0.1 iota_compare_fusion
  6.1 1.3 %fusion = bf16[2,8,16,10,16]{4,3,2,0,1:T(8,128)(2,1)S(1)} fusion(bf16[2,3,16,16]{3,2,1,0:T(8,128)(2,1)} %param.12, pred[1,8,10]{2,0,1:T(4,128)(4,1)S(1)} %get-tuple-element.13, pred[1,8,10]{2,0,1:T(4,128)(4,1)S(1)} %get-tuple-element.14, pred[1,8,10]{2,0,1:T(4,128)(4,1)S(1)} %iota_compare_fusion.2), kind=kOutput, calls=%fused_computation.1 | convolution fusion | flops 287200 | bytes 85232 | tf_op jit(solution)/shard_map/dja,bdoi->bjoai/dot_general | solution.py:191
  7.3 0.1 fusion.1
  7.5 0.1 reshape.238
  7.6 0.1 copy.19
  7.7 0.2 reshape.239
  7.9 0.1 copy.20
  8.0 0.0 collective-permute-done
  8.0 0.0 copy-done
  8.0 0.1 maximum_select_fusion
  8.2 4.0 %collective-permute-start.1 = (bf16[20,32,3]{2,1,0:T(8,128)(2,1)S(1)}, bf16[20,32,3]{2,1,0:T(8,128)(2,1)S(1)}, u32[]{:S(2)}, u32[]{:S(2)}) collective-permute-start(bf16[20,32,3]{2,1,0:T(8,128)(2,1)S(1)} %get-tuple-element.5), channel_id=1, source_target_pairs={{0,1},{1,2},{2,3},{4,5},{5,6},{6,7},{8,9},{9,10},{10,11},{12,13},{... | collective-permute-start | bytes 11528 | tf_op jit(solution)/shard_map/ppermute | solution.py:17
  12.2 1.9 %collective-permute-start.2 = (bf16[20,32,3]{2,1,0:T(8,128)(2,1)S(1)}, bf16[20,32,3]{2,1,0:T(8,128)(2,1)S(1)}, u32[]{:S(2)}, u32[]{:S(2)}) collective-permute-start(bf16[20,32,3]{2,1,0:T(8,128)(2,1)S(1)} %get-tuple-element.6), channel_id=1, source_target_pairs={{1,0},{2,1},{3,2},{5,4},{6,5},{7,6},{9,8},{10,9},{11,10},{13,12},{... | collective-permute-start | bytes 11528 | tf_op jit(solution)/shard_map/ppermute | solution.py:17
  14.1 0.1 pad_maximum_fusion.2.wst_ref
  14.2 0.0 copy-start.1
  14.2 1.0 %copy.23 = bf16[2,8,16,10,16]{2,1,4,3,0:T(8,128)(2,1)S(1)} copy(bf16[2,8,16,10,16]{4,3,2,0,1:T(8,128)(2,1)S(1)} %fusion) | data formatting | bytes 163840 | tf_op jit(solution)/shard_map/convert_element_type | solution.py:192
  15.2 0.0 copy-start.2
  15.2 0.0 copy-start.3
  15.2 0.0 copy-start.4
  15.2 0.4 convert_element_type.70
  15.7 0.1 copy.25.tw_ref
  15.8 0.0 copy-done.1
  15.8 0.1 reshape.241.wsp_ref
  16.0 0.0 copy-done.2
  16.0 0.1 copy.26.tb_ref
  16.1 0.0 copy-done.3
  16.1 0.1 copy.24.bst_ref
  16.1 0.0 copy-done.4
  16.1 0.1 copy.27.hw_ref
  16.9 0.0 collective-permute-done.1
  16.9 1.9 %collective-permute-done.2 = bf16[20,32,3]{2,1,0:T(8,128)(2,1)S(1)} collective-permute-done((bf16[20,32,3]{2,1,0:T(8,128)(2,1)S(1)}, bf16[20,32,3]{2,1,0:T(8,128)(2,1)S(1)}, u32[]{:S(2)}, u32[]{:S(2)}) %collective-permute-start.2) | collective-permute-done | bytes 3872 | tf_op jit(solution)/shard_map/ppermute | solution.py:17
  18.8 0.4 pad_maximum_fusion
  19.2 0.4 convert_element_type.65
  19.7 23.5 %shard_map.82 = f32[16,1,5120]{2,1,0:T(1,128)S(1)} custom-call(s32[1]{0:T(128)} %bitcast.first_ref, f32[24,5632]{1,0:T(8,128)S(1)} %pad_convert_fusion.vp_ref, f32[2,1,5120]{2,1,0:T(1,128)S(1)} %reshape.243.mask_ref, bf16[128,160]{1,0:T(8,128)(2,1)S(1)} %pad_maximum_fusion.2.wst_ref, f32[16,1]{1,0:T(8,128)S(1)} %copy.24.bst_ref, ...), custom_call_target="tpu_custom_call" | custom-call | tf_op jit(solution)/shard_map/pallas_call | solution.py:202
  43.2 0.8 %slice_reduce_fusion = f32[16,5092]{1,0:T(8,128)S(1)} fusion(f32[16,1,5120]{2,1,0:T(1,128)S(1)} %shard_map.82), kind=kLoop, calls=%fused_computation.3 | loop fusion | bytes 651776 | tf_op jit(solution)/shard_map/slice | solution.py:214
  44.0 0.4 reshape_squeeze.3
  44.4 0.8 %slice_bitcast_fusion = f32[16,1,32,128]{3,2,1,0:T(8,128)} fusion(f32[16,38,134]{2,1,0:T(8,128)S(1)} %reshape_squeeze.3), kind=kLoop, calls=%fused_computation.7 | loop fusion | bytes 524288 | tf_op jit(solution)/shard_map/broadcast_in_dim | solution.py:216
  (10 shorter events, 0.2 us)
Async XLA Ops:
  0.8 7.3 %collective-permute-start = (bf16[4,32,128]{2,1,0:T(8,128)(2,1)S(1)}, bf16[4,32,128]{2,1,0:T(8,128)(2,1)S(1)}, u32[]{:S(2)}, u32[]{:S(2)}) collective-permute-start(bf16[4,32,128]{2,1,0:T(8,128)(2,1)S(1)} %slice_bitcast_fusion.1), channel_id=1, source_target_pairs={{0,4},{4,8},{8,12},{12,16},{16,20},{20,24},{24,28},{1,5},{5,9},{9,... | collective-permute-start | bytes 98312 | tf_op jit(solution)/shard_map/ppermute | solution.py:17
  5.6 2.5 %copy-start = (bf16[16,1,32,128]{3,2,1,0:T(8,128)(2,1)S(1)}, bf16[16,1,32,128]{3,2,1,0:T(8,128)(2,1)}, u32[]{:S(2)}) copy-start(bf16[16,1,32,128]{3,2,1,0:T(8,128)(2,1)} %param.8) | copy-start | bytes 393220
  8.2 8.7 %collective-permute-start.1 = (bf16[20,32,3]{2,1,0:T(8,128)(2,1)S(1)}, bf16[20,32,3]{2,1,0:T(8,128)(2,1)S(1)}, u32[]{:S(2)}, u32[]{:S(2)}) collective-permute-start(bf16[20,32,3]{2,1,0:T(8,128)(2,1)S(1)} %get-tuple-element.5), channel_id=1, source_target_pairs={{0,1},{1,2},{2,3},{4,5},{5,6},{6,7},{8,9},{9,10},{10,11},{12,13},{... | collective-permute-start | bytes 11528 | tf_op jit(solution)/shard_map/ppermute | solution.py:17
  12.2 6.6 %collective-permute-start.2 = (bf16[20,32,3]{2,1,0:T(8,128)(2,1)S(1)}, bf16[20,32,3]{2,1,0:T(8,128)(2,1)S(1)}, u32[]{:S(2)}, u32[]{:S(2)}) collective-permute-start(bf16[20,32,3]{2,1,0:T(8,128)(2,1)S(1)} %get-tuple-element.6), channel_id=1, source_target_pairs={{1,0},{2,1},{3,2},{5,4},{6,5},{7,6},{9,8},{10,9},{11,10},{13,12},{... | collective-permute-start | bytes 11528 | tf_op jit(solution)/shard_map/ppermute | solution.py:17
  14.2 1.6 %copy-start.1 = (bf16[2,9,16,16]{3,2,1,0:T(8,128)(2,1)S(1)}, bf16[2,9,16,16]{3,2,1,0:T(8,128)(2,1)}, u32[]{:S(2)}) copy-start(bf16[2,9,16,16]{3,2,1,0:T(8,128)(2,1)} %param.11) | copy-start | bytes 27652
  15.2 0.8 %copy-start.2 = (f32[2,16]{1,0:T(2,128)S(1)}, f32[2,16]{1,0:T(2,128)}, u32[]{:S(2)}) copy-start(f32[2,16]{1,0:T(2,128)} %param.13) | copy-start | bytes 388
  15.2 0.8 %copy-start.3 = (f32[16]{0:T(128)S(1)}, f32[16]{0:T(128)}, u32[]{:S(2)}) copy-start(f32[16]{0:T(128)} %param.10) | copy-start | bytes 196
  15.2 0.9 %copy-start.4 = (f32[16]{0:T(128)S(1)}, f32[16]{0:T(128)}, u32[]{:S(2)}) copy-start(f32[16]{0:T(128)} %param.14) | copy-start | bytes 196

commit v5 on v4

--- a/solution.py
+++ b/solution.py
@@ -7,6 +7,7 @@
 
 HALO = 3
 LEAD = 4
+SPATIAL_GROUP = 4
 
 
 def shifted(value, axis, steps):
@@ -112,19 +113,22 @@
             lo_y, hi_y = wide
             width_y = hi_y - lo_y
             dx_shifts = [(-(base + dx - 1)) % total for dx in range(3)]
-
-            def body(f, carry):
-                x = src_ref[f]
-                pieces = [pltpu.roll(x, sh, 1)[:, lo_y:hi_y] for sh in dx_shifts]
+            a, b = lo - lo_y, hi - lo_y
+            rows = 3 * channels
+            for g0 in range(0, n, SPATIAL_GROUP):
+                frames = [min(g0 + j, n - 1) for j in range(SPATIAL_GROUP)]
+                pieces = []
+                for f in frames:
+                    x = src_ref[f]
+                    pieces += [pltpu.roll(x, sh, 1)[:, lo_y:hi_y] for sh in dx_shifts]
                 patches = jnp.concatenate(pieces, axis=0)
                 y = jnp.dot(wsp_ref[block], patches, preferred_element_type=jnp.float32)
-                a, b = lo - lo_y, hi - lo_y
-                up = pltpu.roll(y[0:channels], pitch, 1)[:, a:b]
-                down = pltpu.roll(y[2 * channels:3 * channels], width_y - pitch, 1)[:, a:b]
-                acc = up + y[channels:2 * channels, a:b] + down
-                s_ref[f, :, lo:hi] = acc.astype(jnp.bfloat16)
-                return carry
-            lax.fori_loop(0, n, body, 0)
+                for j in range(min(SPATIAL_GROUP, n - g0)):
+                    part = y[j * rows:(j + 1) * rows]
+                    up = pltpu.roll(part[0:channels], pitch, 1)[:, a:b]
+                    down = pltpu.roll(part[2 * channels:3 * channels], width_y - pitch, 1)[:, a:b]
+                    acc = up + part[channels:2 * channels, a:b] + down
+                    s_ref[g0 + j, :, lo:hi] = acc.astype(jnp.bfloat16)
 
         def temporal(block, src_ref, n_out, lo, hi, finish):
             for k0 in range(0, n_out, group):
@@ -187,6 +191,8 @@
     bst = stem_bias.astype(jnp.float32)[:, None]
     wsp = spatial_weight.reshape(2, 3, 3, channels, channels).transpose(0, 1, 3, 2, 4)
     wsp = wsp.reshape(2, 3 * channels, 3 * channels)
+    wsp = jnp.einsum("jk,bmn->bjmkn", jnp.eye(SPATIAL_GROUP, dtype=jnp.float32), wsp.astype(jnp.float32))
+    wsp = wsp.reshape(2, SPATIAL_GROUP * 3 * channels, SPATIAL_GROUP * 3 * channels).astype(jnp.bfloat16)
     band = jnp.stack([jnp.eye(8, 10, d, dtype=jnp.float32) for d in range(3)])
     tw = jnp.einsum("dja,bdoi->bjoai", band, temporal_weight.astype(jnp.float32))
     tw = tw.reshape(2, 8 * channels, 10 * channels).astype(jnp.bfloat16)

time: 45.6 us -> 40.3 us (0.88)
  Pallas kernels: 23.5 us -> 17.7 us
  local copies, waits for them, and re-layouts: 5.7 us -> 6.85 us
  matrix products: 1.27 us -> 0.53 us
    pallas_call x1, Pallas kernels: 23.5 us -> 17.7 us  [shards(): pl.pallas_call(make_kernel(n_in, count, pitch, length, base, total, heigh...]
    another operation x1 -> x3, local copies, waits for them, and re-layouts: 0.01 us -> 1.07 us
    dot_general x1, matrix products: 1.27 us -> 0.53 us  [shards(): jnp.einsum('dja,bdoi->bjoai', band, temporal_weight.astype(jnp.float32))]
  transfers between devices with their start and end apart: 3 -> 3, of which waited for: 1 -> 1; matrix products, arithmetic and copies ran while one was open for 11% -> 15% of each run, Pallas kernels for 0% -> 0%
where the time goes in v5:
time: 40.3 us; the launch traced here: 40 us
  Pallas kernels  17.7 us (44%)
  starting transfers between devices  9.84 us (24%)
  local copies, waits for them, and re-layouts  6.85 us (17%)
  other arithmetic  2.23 us (6%)
  waiting for transfers between devices  1.85 us (5%)
  between operations  1 us (2%)
  matrix products  0.53 us (1%)
    pallas_call x1, Pallas kernels, shards(): pl.pallas_call(make_kernel(n_in, count, pitch, length, base, total, heigh...  17.7 us
    ppermute x3, starting transfers between devices, shifted(): lax.ppermute(value, axis, [(source, source + steps) for source in range(l...  9.84 us
    ppermute x3, waiting for transfers between devices, shifted(): lax.ppermute(value, axis, [(source, source + steps) for source in range(l...  1.85 us
    convert_element_type x3, local copies, waits for them, and re-layouts, shards(): tw = tw.reshape(2, 8 * channels, 10 * channels).astype(jnp.bfloat16)  1.49 us
    another operation x3, local copies, waits for them, and re-layouts  1.07 us
    broadcast_in_dim x1, local copies, waits for them, and re-layouts, shards(): return result[:, None]  0.84 us
    slice x1, local copies, waits for them, and re-layouts, shards(): result = out[:, 0, :rows * pitch].reshape(count, rows, pitch)  0.83 us
  transfers between devices with their start and end apart: 3, of which 1 were waited for; matrix products, arithmetic and copies ran while one was open for 15% of the time, Pallas kernels for 0%

profile of v5, /device:TPU:1, one launch (start us, length us, event | category | flops | bytes accessed | tf_op | source)
XLA Modules:
  0.0 40.0 jit_solution(2789116044603483110)
XLA Ops:
  0.0 0.0 copy-start.1
  0.0 0.8 %slice_bitcast_fusion.1 = bf16[4,32,128]{2,1,0:T(8,128)(2,1)S(1)} fusion(bf16[16,1,32,128]{3,2,0,1:T(8,128)(2,1)} %bitcast.48), kind=kLoop, calls=%fused_computation.26 | loop fusion | bytes 65536 | tf_op jit(solution)/shard_map/slice | solution.py:168
  0.8 3.9 %collective-permute-start = (bf16[4,32,128]{2,1,0:T(8,128)(2,1)S(1)}, bf16[4,32,128]{2,1,0:T(8,128)(2,1)S(1)}, u32[]{:S(2)}, u32[]{:S(2)}) collective-permute-start(bf16[4,32,128]{2,1,0:T(8,128)(2,1)S(1)} %slice_bitcast_fusion.1), channel_id=1, source_target_pairs={{0,4},{4,8},{8,12},{12,16},{16,20},{20,24},{24,28},{1,5},{5,9},{9,... | collective-permute-start | bytes 98312 | tf_op jit(solution)/shard_map/ppermute | solution.py:18
  4.8 0.8 %convert_convert_fusion = (f32[9,16]{1,0:T(8,128)S(1)}, f32[9,16]{1,0:T(8,128)S(1)}) fusion(f32[9,16]{1,0:T(8,128)} %param.9), kind=kLoop, calls=%fused_computation.39 | loop fusion | flops 432 | bytes 1728 | tf_op jit(solution)/shard_map/convert_element_type | solution.py:182
  5.6 0.9 %copy.34 = f32[2,3,3,16,16]{4,2,3,1,0:T(4,128)S(1)} copy(bf16[2,3,3,16,16]{4,3,2,1,0:T(8,128)(2,1)} %bitcast.51) | data formatting | bytes 27648 | tf_op jit(solution)/shard_map/convert.14
  6.5 0.1 reshape.250
  6.7 0.3 compare_and_fusion
  7.0 0.1 add_convert_fusion
  7.0 0.1 iota_compare_fusion
  7.1 0.2 fusion.1
  7.3 0.0 copy-start
  7.3 0.0 copy-done.1
  7.4 0.5 %fusion = bf16[2,8,16,10,16]{4,3,2,0,1:T(8,128)(2,1)S(1)} fusion(bf16[2,3,16,16]{3,2,1,0:T(8,128)(2,1)S(1)} %copy-done.1, pred[1,8,10]{2,0,1:T(4,128)(4,1)S(1)} %get-tuple-element.13, pred[1,8,10]{2,0,1:T(4,128)(4,1)S(1)} %get-tuple-element.14, pred[1,8,10]{2,0,1:T(4,128)(4,1)S(1)} %iota_compare_fusion.2), kind=kOutput, calls=%fused_computation.1 | convolution fusion | flops 287200 | bytes 85232 | tf_op jit(solution)/shard_map/dja,bdoi->bjoai/dot_general | solution.py:197
  7.9 0.1 fusion.2
  8.0 0.1 reshape.244
  8.2 0.1 copy.18
  8.3 0.2 reshape.245
  8.5 0.1 copy.19
  8.6 0.0 collective-permute-done
  8.6 0.0 copy-done
  8.6 0.1 maximum_select_fusion
  8.7 4.0 %collective-permute-start.1 = (bf16[20,32,3]{2,1,0:T(8,128)(2,1)S(1)}, bf16[20,32,3]{2,1,0:T(8,128)(2,1)S(1)}, u32[]{:S(2)}, u32[]{:S(2)}) collective-permute-start(bf16[20,32,3]{2,1,0:T(8,128)(2,1)S(1)} %get-tuple-element.5), channel_id=1, source_target_pairs={{0,1},{1,2},{2,3},{4,5},{5,6},{6,7},{8,9},{9,10},{10,11},{12,13},{... | collective-permute-start | bytes 11528 | tf_op jit(solution)/shard_map/ppermute | solution.py:18
  12.7 1.9 %collective-permute-start.2 = (bf16[20,32,3]{2,1,0:T(8,128)(2,1)S(1)}, bf16[20,32,3]{2,1,0:T(8,128)(2,1)S(1)}, u32[]{:S(2)}, u32[]{:S(2)}) collective-permute-start(bf16[20,32,3]{2,1,0:T(8,128)(2,1)S(1)} %get-tuple-element.6), channel_id=1, source_target_pairs={{1,0},{2,1},{3,2},{5,4},{6,5},{7,6},{9,8},{10,9},{11,10},{13,12},{... | collective-permute-start | bytes 11528 | tf_op jit(solution)/shard_map/ppermute | solution.py:18
  14.7 0.1 pad_maximum_fusion.2.wst_ref
  14.8 1.0 %copy.22 = bf16[2,8,16,10,16]{2,1,4,3,0:T(8,128)(2,1)S(1)} copy(bf16[2,8,16,10,16]{4,3,2,0,1:T(8,128)(2,1)S(1)} %fusion) | data formatting | bytes 163840 | tf_op jit(solution)/shard_map/convert_element_type | solution.py:198
  15.7 0.0 copy-start.2
  15.8 0.0 copy-start.3
  15.8 0.0 copy-start.4
  15.8 0.4 %convert_element_type.82 = bf16[2,128,160]{1,2,0:T(8,128)(2,1)S(1)} reshape(bf16[2,8,16,10,16]{2,1,4,3,0:T(8,128)(2,1)S(1)} %copy.22) | data formatting | bytes 163840 | tf_op jit(solution)/shard_map/convert_element_type | solution.py:198
  16.2 0.1 copy.24.tw_ref
  16.3 0.2 convert_element_type.79.wsp_ref
  16.6 0.0 copy-done.2
  16.6 0.1 copy.25.tb_ref
  16.7 0.0 copy-done.3
  16.7 0.1 copy.23.bst_ref
  16.8 0.0 copy-done.4
  16.8 0.1 copy.26.hw_ref
  17.5 0.0 collective-permute-done.1
  17.5 1.8 %collective-permute-done.2 = bf16[20,32,3]{2,1,0:T(8,128)(2,1)S(1)} collective-permute-done((bf16[20,32,3]{2,1,0:T(8,128)(2,1)S(1)}, bf16[20,32,3]{2,1,0:T(8,128)(2,1)S(1)}, u32[]{:S(2)}, u32[]{:S(2)}) %collective-permute-start.2) | collective-permute-done | bytes 3872 | tf_op jit(solution)/shard_map/ppermute | solution.py:18
  19.4 0.4 %pad_maximum_fusion = bf16[20,38,134]{2,1,0:T(8,128)(2,1)S(1)} fusion(bf16[20,3,134]{2,1,0:T(4,128)(2,1)S(1)} %broadcast.307, bf16[20,32,3]{2,1,0:T(8,128)(2,1)S(1)} %collective-permute-done.2, bf16[16,32,128]{2,1,0:T(8,128)(2,1)S(1)} %bitcast.50, bf16[4,32,128]{2,1,0:T(8,128)(2,1)S(1)} %collective-permute-done, bf16[20,32,3]{2,1,0:T(8,128)(2,1)S(1)} %collective-permute-done.1), kind=kLoop, calls=%fused_computation.3 | loop fusion | flops 1222080 | bytes 391280 | tf_op jit(solution)/shard_map/concatenate | solution.py:39
  19.8 0.4 convert_element_type.74
  20.2 17.7 %shard_map.82 = f32[16,1,5120]{2,1,0:T(1,128)S(1)} custom-call(s32[1]{0:T(128)} %bitcast.first_ref, f32[24,5632]{1,0:T(8,128)S(1)} %pad_convert_fusion.vp_ref, f32[2,1,5120]{2,1,0:T(1,128)S(1)} %reshape.249.mask_ref, bf16[128,160]{1,0:T(8,128)(2,1)S(1)} %pad_maximum_fusion.2.wst_ref, f32[16,1]{1,0:T(8,128)S(1)} %copy.23.bst_ref, ...), custom_call_target="tpu_custom_call" | custom-call | tf_op jit(solution)/shard_map/pallas_call | solution.py:208
  37.9 0.8 %slice_reduce_fusion = f32[16,5092]{1,0:T(8,128)S(1)} fusion(f32[16,1,5120]{2,1,0:T(1,128)S(1)} %shard_map.82), kind=kLoop, calls=%fused_computation.5 | loop fusion | bytes 651776 | tf_op jit(solution)/shard_map/slice | solution.py:220
  38.8 0.4 reshape_squeeze.3
  39.1 0.8 %slice_bitcast_fusion = f32[16,1,32,128]{3,2,1,0:T(8,128)} fusion(f32[16,38,134]{2,1,0:T(8,128)S(1)} %reshape_squeeze.3), kind=kLoop, calls=%fused_computation.9 | loop fusion | bytes 524288 | tf_op jit(solution)/shard_map/broadcast_in_dim | solution.py:222
  (10 shorter events, 0.1 us)
Async XLA Ops:
  0.0 7.3 %copy-start.1 = (bf16[2,3,16,16]{3,2,1,0:T(8,128)(2,1)S(1)}, bf16[2,3,16,16]{3,2,1,0:T(8,128)(2,1)}, u32[]{:S(2)}) copy-start(bf16[2,3,16,16]{3,2,1,0:T(8,128)(2,1)} %param.12) | copy-start | bytes 9220
  0.8 7.8 %collective-permute-start = (bf16[4,32,128]{2,1,0:T(8,128)(2,1)S(1)}, bf16[4,32,128]{2,1,0:T(8,128)(2,1)S(1)}, u32[]{:S(2)}, u32[]{:S(2)}) collective-permute-start(bf16[4,32,128]{2,1,0:T(8,128)(2,1)S(1)} %slice_bitcast_fusion.1), channel_id=1, source_target_pairs={{0,4},{4,8},{8,12},{12,16},{16,20},{20,24},{24,28},{1,5},{5,9},{9,... | collective-permute-start | bytes 98312 | tf_op jit(solution)/shard_map/ppermute | solution.py:18
  7.3 1.3 %copy-start = (bf16[16,1,32,128]{3,2,1,0:T(8,128)(2,1)S(1)}, bf16[16,1,32,128]{3,2,1,0:T(8,128)(2,1)}, u32[]{:S(2)}) copy-start(bf16[16,1,32,128]{3,2,1,0:T(8,128)(2,1)} %param.8) | copy-start | bytes 393220
  8.7 8.8 %collective-permute-start.1 = (bf16[20,32,3]{2,1,0:T(8,128)(2,1)S(1)}, bf16[20,32,3]{2,1,0:T(8,128)(2,1)S(1)}, u32[]{:S(2)}, u32[]{:S(2)}) collective-permute-start(bf16[20,32,3]{2,1,0:T(8,128)(2,1)S(1)} %get-tuple-element.5), channel_id=1, source_target_pairs={{0,1},{1,2},{2,3},{4,5},{5,6},{6,7},{8,9},{9,10},{10,11},{12,13},{... | collective-permute-start | bytes 11528 | tf_op jit(solution)/shard_map/ppermute | solution.py:18
  12.7 6.6 %collective-permute-start.2 = (bf16[20,32,3]{2,1,0:T(8,128)(2,1)S(1)}, bf16[20,32,3]{2,1,0:T(8,128)(2,1)S(1)}, u32[]{:S(2)}, u32[]{:S(2)}) collective-permute-start(bf16[20,32,3]{2,1,0:T(8,128)(2,1)S(1)} %get-tuple-element.6), channel_id=1, source_target_pairs={{1,0},{2,1},{3,2},{5,4},{6,5},{7,6},{9,8},{10,9},{11,10},{13,12},{... | collective-permute-start | bytes 11528 | tf_op jit(solution)/shard_map/ppermute | solution.py:18
  15.7 0.8 %copy-start.2 = (f32[2,16]{1,0:T(2,128)S(1)}, f32[2,16]{1,0:T(2,128)}, u32[]{:S(2)}) copy-start(f32[2,16]{1,0:T(2,128)} %param.13) | copy-start | bytes 388
  15.8 0.9 %copy-start.3 = (f32[16]{0:T(128)S(1)}, f32[16]{0:T(128)}, u32[]{:S(2)}) copy-start(f32[16]{0:T(128)} %param.10) | copy-start | bytes 196
  15.8 1.0 %copy-start.4 = (f32[16]{0:T(128)S(1)}, f32[16]{0:T(128)}, u32[]{:S(2)}) copy-start(f32[16]{0:T(128)} %param.14) | copy-start | bytes 196

commit v6 on v5

--- a/solution.py
+++ b/solution.py
@@ -155,7 +155,7 @@
 
         def finish1(k, h2):
             head = jnp.sum(hw_ref[...] * h2.astype(jnp.float32), axis=0, keepdims=True) + hb_ref[...]
-            out_ref[k, :, lo2:hi2] = head
+            out_ref[k:k + 1, lo2:hi2] = head
 
         temporal(1, hb2_ref, count, lo2, hi2, finish1)
 
@@ -207,7 +207,7 @@
     spec = pl.BlockSpec(memory_space=vmem)
     out = pl.pallas_call(
         make_kernel(n_in, count, pitch, length, base, total, height),
-        out_shape=jax.ShapeDtypeStruct((count, 1, length), jnp.float32),
+        out_shape=jax.ShapeDtypeStruct((count, length), jnp.float32),
         in_specs=[pl.BlockSpec(memory_space=smem)] + [spec] * 9,
         out_specs=spec,
         scratch_shapes=[
@@ -217,7 +217,7 @@
         ],
         compiler_params=pltpu.CompilerParams(vmem_limit_bytes=48 * 1024 * 1024),
     )(first, vp, masks, wst, bst, wsp, tw, tb, hw, hb)
-    result = out[:, 0, : rows * pitch].reshape(count, rows, pitch)
+    result = out[:, : rows * pitch].reshape(count, rows, pitch)
     result = result[:, HALO:HALO + height, HALO:HALO + width]
     return result[:, None]
 

time: 40.3 us -> 39.5 us (0.980)
  local copies, waits for them, and re-layouts: 6.85 us -> 6.02 us
    slice x1 -> x0, local copies, waits for them, and re-layouts: 0.83 us -> none  [shards(): result = out[:, 0, :rows * pitch].reshape(count, rows, pitch)]
    another operation x4 -> x3, local copies, waits for them, and re-layouts: 1.45 us -> 1.07 us
where the time goes in v6:
time: 39.5 us; the launch traced here: 39.2 us
  Pallas kernels  17.7 us (45%)
  starting transfers between devices  9.84 us (25%)
  local copies, waits for them, and re-layouts  6.02 us (15%)
  other arithmetic  2.23 us (6%)
  waiting for transfers between devices  1.85 us (5%)
  between operations  0.99 us (3%)
  matrix products  0.53 us (1%)
    pallas_call x1, Pallas kernels, shards(): pl.pallas_call(make_kernel(n_in, count, pitch, length, base, total, heigh...  17.7 us
    ppermute x3, starting transfers between devices, shifted(): lax.ppermute(value, axis, [(source, source + steps) for source in range(l...  9.84 us
    ppermute x3, waiting for transfers between devices, shifted(): lax.ppermute(value, axis, [(source, source + steps) for source in range(l...  1.85 us
    convert_element_type x3, local copies, waits for them, and re-layouts, shards(): tw = tw.reshape(2, 8 * channels, 10 * channels).astype(jnp.bfloat16)  1.48 us
    another operation x3, local copies, waits for them, and re-layouts  1.07 us
    broadcast_in_dim x1, local copies, waits for them, and re-layouts, shards(): return result[:, None]  0.84 us
  transfers between devices with their start and end apart: 3, of which 1 were waited for; matrix products, arithmetic and copies ran while one was open for 15% of the time, Pallas kernels for 0%

profile of v6, /device:TPU:1, one launch (start us, length us, event | category | flops | bytes accessed | tf_op | source)
XLA Modules:
  0.0 39.2 jit_solution(704140412784061047)
XLA Ops:
  0.0 0.0 copy-start.1
  0.0 0.8 %slice_bitcast_fusion.1 = bf16[4,32,128]{2,1,0:T(8,128)(2,1)S(1)} fusion(bf16[16,1,32,128]{3,2,0,1:T(8,128)(2,1)} %bitcast.50), kind=kLoop, calls=%fused_computation.25 | loop fusion | bytes 65536 | tf_op jit(solution)/shard_map/slice | solution.py:168
  0.8 3.9 %collective-permute-start = (bf16[4,32,128]{2,1,0:T(8,128)(2,1)S(1)}, bf16[4,32,128]{2,1,0:T(8,128)(2,1)S(1)}, u32[]{:S(2)}, u32[]{:S(2)}) collective-permute-start(bf16[4,32,128]{2,1,0:T(8,128)(2,1)S(1)} %slice_bitcast_fusion.1), channel_id=1, source_target_pairs={{0,4},{4,8},{8,12},{12,16},{16,20},{20,24},{24,28},{1,5},{5,9},{9,... | collective-permute-start | bytes 98312 | tf_op jit(solution)/shard_map/ppermute | solution.py:18
  4.8 0.8 %convert_convert_fusion = (f32[9,16]{1,0:T(8,128)S(1)}, f32[9,16]{1,0:T(8,128)S(1)}) fusion(f32[9,16]{1,0:T(8,128)} %param.9), kind=kLoop, calls=%fused_computation.38 | loop fusion | flops 432 | bytes 1728 | tf_op jit(solution)/shard_map/convert_element_type | solution.py:182
  5.6 0.9 %copy.34 = f32[2,3,3,16,16]{4,2,3,1,0:T(4,128)S(1)} copy(bf16[2,3,3,16,16]{4,3,2,1,0:T(8,128)(2,1)} %bitcast.53) | data formatting | bytes 27648 | tf_op jit(solution)/shard_map/convert.14
  6.5 0.1 reshape.254
  6.7 0.3 compare_and_fusion
  7.0 0.1 add_convert_fusion
  7.0 0.1 iota_compare_fusion
  7.1 0.2 fusion.1
  7.3 0.0 copy-start
  7.3 0.0 copy-done.1
  7.4 0.5 %fusion = bf16[2,8,16,10,16]{4,3,2,0,1:T(8,128)(2,1)S(1)} fusion(bf16[2,3,16,16]{3,2,1,0:T(8,128)(2,1)S(1)} %copy-done.1, pred[1,8,10]{2,0,1:T(4,128)(4,1)S(1)} %get-tuple-element.13, pred[1,8,10]{2,0,1:T(4,128)(4,1)S(1)} %get-tuple-element.14, pred[1,8,10]{2,0,1:T(4,128)(4,1)S(1)} %iota_compare_fusion.2), kind=kOutput, calls=%fused_computation.1 | convolution fusion | flops 287200 | bytes 85232 | tf_op jit(solution)/shard_map/dja,bdoi->bjoai/dot_general | solution.py:197
  7.9 0.1 fusion.2
  8.0 0.1 reshape.247
  8.2 0.1 copy.18
  8.3 0.2 reshape.248
  8.5 0.1 copy.19
  8.6 0.0 collective-permute-done
  8.6 0.0 copy-done
  8.6 0.1 maximum_select_fusion
  8.7 4.0 %collective-permute-start.1 = (bf16[20,32,3]{2,1,0:T(8,128)(2,1)S(1)}, bf16[20,32,3]{2,1,0:T(8,128)(2,1)S(1)}, u32[]{:S(2)}, u32[]{:S(2)}) collective-permute-start(bf16[20,32,3]{2,1,0:T(8,128)(2,1)S(1)} %get-tuple-element.5), channel_id=1, source_target_pairs={{0,1},{1,2},{2,3},{4,5},{5,6},{6,7},{8,9},{9,10},{10,11},{12,13},{... | collective-permute-start | bytes 11528 | tf_op jit(solution)/shard_map/ppermute | solution.py:18
  12.7 1.9 %collective-permute-start.2 = (bf16[20,32,3]{2,1,0:T(8,128)(2,1)S(1)}, bf16[20,32,3]{2,1,0:T(8,128)(2,1)S(1)}, u32[]{:S(2)}, u32[]{:S(2)}) collective-permute-start(bf16[20,32,3]{2,1,0:T(8,128)(2,1)S(1)} %get-tuple-element.6), channel_id=1, source_target_pairs={{1,0},{2,1},{3,2},{5,4},{6,5},{7,6},{9,8},{10,9},{11,10},{13,12},{... | collective-permute-start | bytes 11528 | tf_op jit(solution)/shard_map/ppermute | solution.py:18
  14.7 0.1 pad_maximum_fusion.2.wst_ref
  14.8 1.0 %copy.22 = bf16[2,8,16,10,16]{2,1,4,3,0:T(8,128)(2,1)S(1)} copy(bf16[2,8,16,10,16]{4,3,2,0,1:T(8,128)(2,1)S(1)} %fusion) | data formatting | bytes 163840 | tf_op jit(solution)/shard_map/convert_element_type | solution.py:198
  15.7 0.0 copy-start.2
  15.8 0.0 copy-start.3
  15.8 0.0 copy-start.4
  15.8 0.4 %convert_element_type.82 = bf16[2,128,160]{1,2,0:T(8,128)(2,1)S(1)} reshape(bf16[2,8,16,10,16]{2,1,4,3,0:T(8,128)(2,1)S(1)} %copy.22) | data formatting | bytes 163840 | tf_op jit(solution)/shard_map/convert_element_type | solution.py:198
  16.2 0.1 copy.24.tw_ref
  16.3 0.2 convert_element_type.79.wsp_ref
  16.6 0.0 copy-done.2
  16.6 0.1 copy.25.tb_ref
  16.7 0.0 copy-done.3
  16.7 0.1 copy.23.bst_ref
  16.8 0.0 copy-done.4
  16.8 0.1 copy.26.hw_ref
  17.5 0.0 collective-permute-done.1
  17.5 1.8 %collective-permute-done.2 = bf16[20,32,3]{2,1,0:T(8,128)(2,1)S(1)} collective-permute-done((bf16[20,32,3]{2,1,0:T(8,128)(2,1)S(1)}, bf16[20,32,3]{2,1,0:T(8,128)(2,1)S(1)}, u32[]{:S(2)}, u32[]{:S(2)}) %collective-permute-start.2) | collective-permute-done | bytes 3872 | tf_op jit(solution)/shard_map/ppermute | solution.py:18
  19.4 0.4 %pad_maximum_fusion = bf16[20,38,134]{2,1,0:T(8,128)(2,1)S(1)} fusion(bf16[20,3,134]{2,1,0:T(4,128)(2,1)S(1)} %broadcast.307, bf16[20,32,3]{2,1,0:T(8,128)(2,1)S(1)} %collective-permute-done.2, bf16[16,32,128]{2,1,0:T(8,128)(2,1)S(1)} %bitcast.52, bf16[4,32,128]{2,1,0:T(8,128)(2,1)S(1)} %collective-permute-done, bf16[20,32,3]{2,1,0:T(8,128)(2,1)S(1)} %collective-permute-done.1), kind=kLoop, calls=%fused_computation.3 | loop fusion | flops 1222080 | bytes 391280 | tf_op jit(solution)/shard_map/concatenate | solution.py:39
  19.8 0.4 convert_element_type.74
  20.2 17.7 %shard_map.82 = f32[16,5120]{1,0:T(8,128)S(1)} custom-call(s32[1]{0:T(128)} %bitcast.first_ref, f32[24,5632]{1,0:T(8,128)S(1)} %pad_convert_fusion.vp_ref, f32[2,1,5120]{2,1,0:T(1,128)S(1)} %reshape.253.mask_ref, bf16[128,160]{1,0:T(8,128)(2,1)S(1)} %pad_maximum_fusion.2.wst_ref, f32[16,1]{1,0:T(8,128)S(1)} %copy.23.bst_ref, ...), custom_call_target="tpu_custom_call" | custom-call | tf_op jit(solution)/shard_map/pallas_call | solution.py:208
  37.9 0.4 reshape.252
  38.3 0.8 %slice_bitcast_fusion = f32[16,1,32,128]{3,2,1,0:T(8,128)} fusion(f32[16,38,134]{2,1,0:T(8,128)S(1)} %reshape.252), kind=kLoop, calls=%fused_computation.8 | loop fusion | bytes 524288 | tf_op jit(solution)/shard_map/broadcast_in_dim | solution.py:222
  (10 shorter events, 0.1 us)
Async XLA Ops:
  0.0 7.3 %copy-start.1 = (bf16[2,3,16,16]{3,2,1,0:T(8,128)(2,1)S(1)}, bf16[2,3,16,16]{3,2,1,0:T(8,128)(2,1)}, u32[]{:S(2)}) copy-start(bf16[2,3,16,16]{3,2,1,0:T(8,128)(2,1)} %param.12) | copy-start | bytes 9220
  0.8 7.8 %collective-permute-start = (bf16[4,32,128]{2,1,0:T(8,128)(2,1)S(1)}, bf16[4,32,128]{2,1,0:T(8,128)(2,1)S(1)}, u32[]{:S(2)}, u32[]{:S(2)}) collective-permute-start(bf16[4,32,128]{2,1,0:T(8,128)(2,1)S(1)} %slice_bitcast_fusion.1), channel_id=1, source_target_pairs={{0,4},{4,8},{8,12},{12,16},{16,20},{20,24},{24,28},{1,5},{5,9},{9,... | collective-permute-start | bytes 98312 | tf_op jit(solution)/shard_map/ppermute | solution.py:18
  7.3 1.3 %copy-start = (bf16[16,1,32,128]{3,2,1,0:T(8,128)(2,1)S(1)}, bf16[16,1,32,128]{3,2,1,0:T(8,128)(2,1)}, u32[]{:S(2)}) copy-start(bf16[16,1,32,128]{3,2,1,0:T(8,128)(2,1)} %param.8) | copy-start | bytes 393220
  8.7 8.8 %collective-permute-start.1 = (bf16[20,32,3]{2,1,0:T(8,128)(2,1)S(1)}, bf16[20,32,3]{2,1,0:T(8,128)(2,1)S(1)}, u32[]{:S(2)}, u32[]{:S(2)}) collective-permute-start(bf16[20,32,3]{2,1,0:T(8,128)(2,1)S(1)} %get-tuple-element.5), channel_id=1, source_target_pairs={{0,1},{1,2},{2,3},{4,5},{5,6},{6,7},{8,9},{9,10},{10,11},{12,13},{... | collective-permute-start | bytes 11528 | tf_op jit(solution)/shard_map/ppermute | solution.py:18
  12.7 6.6 %collective-permute-start.2 = (bf16[20,32,3]{2,1,0:T(8,128)(2,1)S(1)}, bf16[20,32,3]{2,1,0:T(8,128)(2,1)S(1)}, u32[]{:S(2)}, u32[]{:S(2)}) collective-permute-start(bf16[20,32,3]{2,1,0:T(8,128)(2,1)S(1)} %get-tuple-element.6), channel_id=1, source_target_pairs={{1,0},{2,1},{3,2},{5,4},{6,5},{7,6},{9,8},{10,9},{11,10},{13,12},{... | collective-permute-start | bytes 11528 | tf_op jit(solution)/shard_map/ppermute | solution.py:18
  15.7 0.8 %copy-start.2 = (f32[2,16]{1,0:T(2,128)S(1)}, f32[2,16]{1,0:T(2,128)}, u32[]{:S(2)}) copy-start(f32[2,16]{1,0:T(2,128)} %param.13) | copy-start | bytes 388
  15.8 0.9 %copy-start.3 = (f32[16]{0:T(128)S(1)}, f32[16]{0:T(128)}, u32[]{:S(2)}) copy-start(f32[16]{0:T(128)} %param.10) | copy-start | bytes 196
  15.8 1.0 %copy-start.4 = (f32[16]{0:T(128)S(1)}, f32[16]{0:T(128)}, u32[]{:S(2)}) copy-start(f32[16]{0:T(128)} %param.14) | copy-start | bytes 196

commit v7 on v6

--- a/solution.py
+++ b/solution.py
@@ -134,11 +134,18 @@
             for k0 in range(0, n_out, group):
                 stacked = jnp.concatenate([s_ref[k0 + jj, :, lo:hi] for jj in range(group + 2)], axis=0)
                 acc = jnp.dot(tw_ref[block], stacked, preferred_element_type=jnp.float32)
+                done = []
                 for j in range(min(group, n_out - k0)):
                     k = k0 + j
                     part = acc[j * channels:(j + 1) * channels] + tb_ref[block]
                     centre = src_ref[k + 2, :, base + lo:base + hi].astype(jnp.float32)
-                    finish(k, (centre + jnp.maximum(part, 0.0)).astype(jnp.bfloat16))
+                    done.append(finish(k, (centre + jnp.maximum(part, 0.0)).astype(jnp.bfloat16)))
+                if done[0] is not None:
+                    done += [jnp.zeros_like(done[0])] * (group - len(done))
+                    stacked_h = jnp.concatenate(done, axis=0)
+                    heads = jnp.dot(hw_ref[...], jnp.concatenate([stacked_h, stacked_h], axis=0),
+                                    preferred_element_type=jnp.float32) + hb_ref[...]
+                    out_ref[k0:k0 + group, lo:hi] = heads
 
         s_ref[n_in:, :, :] = jnp.zeros((s_ref.shape[0] - n_in, channels, length), jnp.bfloat16)
         lo1, hi1 = spans[1]
@@ -154,8 +161,7 @@
         spatial(1, hb2_ref, n_in - 2, spans[1], lo2, hi2)
 
         def finish1(k, h2):
-            head = jnp.sum(hw_ref[...] * h2.astype(jnp.float32), axis=0, keepdims=True) + hb_ref[...]
-            out_ref[k:k + 1, lo2:hi2] = head
+            return h2
 
         temporal(1, hb2_ref, count, lo2, hi2, finish1)
 
@@ -197,7 +203,11 @@
     tw = jnp.einsum("dja,bdoi->bjoai", band, temporal_weight.astype(jnp.float32))
     tw = tw.reshape(2, 8 * channels, 10 * channels).astype(jnp.bfloat16)
     tb = temporal_bias.astype(jnp.float32)[:, :, None]
-    hw = head_weight.astype(jnp.float32)[:, None]
+    hw_hi = head_weight.astype(jnp.bfloat16).astype(jnp.float32)
+    hw_lo = head_weight - hw_hi
+    frame_eye = jnp.eye(8, dtype=jnp.float32)
+    hw = jnp.concatenate([jnp.einsum("jk,c->jkc", frame_eye, w).reshape(8, 8 * channels) for w in (hw_hi, hw_lo)], axis=1)
+    hw = hw.astype(jnp.bfloat16)
     hb = head_bias.astype(jnp.float32).reshape(1, 1)
     masks = flat_masks(height, width, length)
     first = (lax.axis_index("tm") * count - LEAD).astype(jnp.int32).reshape(1)
@@ -207,7 +217,7 @@
     spec = pl.BlockSpec(memory_space=vmem)
     out = pl.pallas_call(
         make_kernel(n_in, count, pitch, length, base, total, height),
-        out_shape=jax.ShapeDtypeStruct((count, length), jnp.float32),
+        out_shape=jax.ShapeDtypeStruct((round_up(count, 8), length), jnp.float32),
         in_specs=[pl.BlockSpec(memory_space=smem)] + [spec] * 9,
         out_specs=spec,
         scratch_shapes=[
@@ -217,7 +227,7 @@
         ],
         compiler_params=pltpu.CompilerParams(vmem_limit_bytes=48 * 1024 * 1024),
     )(first, vp, masks, wst, bst, wsp, tw, tb, hw, hb)
-    result = out[:, : rows * pitch].reshape(count, rows, pitch)
+    result = out[:count, : rows * pitch].reshape(count, rows, pitch)
     result = result[:, HALO:HALO + height, HALO:HALO + width]
     return result[:, None]
 

time: 39.5 us -> 38.4 us (0.972)
  Pallas kernels: 17.7 us -> 16.3 us
  other arithmetic: 2.23 us -> 3.06 us
  local copies, waits for them, and re-layouts: 6.02 us -> 5.35 us
    pallas_call x1, Pallas kernels: 17.7 us -> 16.3 us  [shards(): pl.pallas_call(make_kernel(n_in, count, pitch, length, base, total, heigh...]
    another operation x2 -> x4, other arithmetic: 0.01 us -> 0.83 us
    another operation x3 -> x4, local copies, waits for them, and re-layouts: 1.07 us -> 0.25 us
  transfers between devices with their start and end apart: 3 -> 3, of which waited for: 1 -> 1; matrix products, arithmetic and copies ran while one was open for 15% -> 16% of each run, Pallas kernels for 0% -> 0%
where the time goes in v7:
time: 38.4 us; the launch traced here: 38.1 us
  Pallas kernels  16.3 us (42%)
  starting transfers between devices  9.84 us (26%)
  local copies, waits for them, and re-layouts  5.35 us (14%)
  other arithmetic  3.06 us (8%)
  waiting for transfers between devices  2.03 us (5%)
  between operations  0.99 us (3%)
  matrix products  0.53 us (1%)
    pallas_call x1, Pallas kernels, shards(): pl.pallas_call(make_kernel(n_in, count, pitch, length, base, total, heigh...  16.3 us
    ppermute x3, starting transfers between devices, shifted(): lax.ppermute(value, axis, [(source, source + steps) for source in range(l...  9.84 us
    ppermute x3, waiting for transfers between devices, shifted(): lax.ppermute(value, axis, [(source, source + steps) for source in range(l...  2.03 us
    convert_element_type x3, local copies, waits for them, and re-layouts, shards(): tw = tw.reshape(2, 8 * channels, 10 * channels).astype(jnp.bfloat16)  1.49 us
    broadcast_in_dim x1, local copies, waits for them, and re-layouts, shards(): return result[:, None]  0.84 us
    another operation x4, other arithmetic  0.83 us
    slice x1, local copies, waits for them, and re-layouts, shards(): lead = shifted(clip[-LEAD:], 'tm', 1)  0.79 us
    convert_element_type x1, other arithmetic, shards(): w_hi = stem_weight.astype(jnp.bfloat16).astype(jnp.float32)  0.78 us
  transfers between devices with their start and end apart: 3, of which 1 were waited for; matrix products, arithmetic and copies ran while one was open for 16% of the time, Pallas kernels for 0%

profile of v7, /device:TPU:1, one launch (start us, length us, event | category | flops | bytes accessed | tf_op | source)
XLA Modules:
  0.0 38.1 jit_solution(16365348547140582985)
XLA Ops:
  0.0 0.0 copy-start.1
  0.0 0.8 %slice_bitcast_fusion.1 = bf16[4,32,128]{2,1,0:T(8,128)(2,1)S(1)} fusion(bf16[16,1,32,128]{3,2,0,1:T(8,128)(2,1)} %bitcast.49), kind=kLoop, calls=%fused_computation.25 | loop fusion | bytes 65536 | tf_op jit(solution)/shard_map/slice | solution.py:174
  0.8 3.9 %collective-permute-start = (bf16[4,32,128]{2,1,0:T(8,128)(2,1)S(1)}, bf16[4,32,128]{2,1,0:T(8,128)(2,1)S(1)}, u32[]{:S(2)}, u32[]{:S(2)}) collective-permute-start(bf16[4,32,128]{2,1,0:T(8,128)(2,1)S(1)} %slice_bitcast_fusion.1), channel_id=1, source_target_pairs={{0,4},{4,8},{8,12},{12,16},{16,20},{20,24},{24,28},{1,5},{5,9},{9,... | collective-permute-start | bytes 98312 | tf_op jit(solution)/shard_map/ppermute | solution.py:18
  4.7 0.0 copy-start.2
  4.8 0.8 %convert_convert_fusion = (f32[9,16]{1,0:T(8,128)S(1)}, f32[9,16]{1,0:T(8,128)S(1)}) fusion(f32[9,16]{1,0:T(8,128)} %param.9), kind=kLoop, calls=%fused_computation.41 | loop fusion | flops 432 | bytes 1728 | tf_op jit(solution)/shard_map/convert_element_type | solution.py:188
  5.6 0.1 copy.22
  5.7 0.1 fusion.2
  5.8 0.1 reshape.255
  6.0 0.1 copy.17
  6.1 0.2 reshape.256
  6.3 0.1 copy.18
  6.4 0.7 %convert_convert_fusion.1 = (f32[16]{0:T(128)S(1)}, f32[16]{0:T(128)S(1)}) fusion(f32[16]{0:T(128)} %param.14), kind=kLoop, calls=%fused_computation.47 | loop fusion | flops 48 | bytes 192 | tf_op jit(solution)/shard_map/convert.5
  7.1 0.0 copy-done.1
  7.2 0.0 copy-start
  7.2 0.1 reshape.264
  7.3 0.3 compare_and_fusion
  7.6 0.1 add_convert_fusion
  7.7 0.1 iota_compare_fusion
  7.8 0.2 fusion.1
  8.0 0.1 multiply_convert_fusion.4
  8.1 0.0 copy-done.2
  8.1 0.5 %fusion = bf16[2,8,16,10,16]{4,3,2,0,1:T(8,128)(2,1)S(1)} fusion(bf16[2,3,16,16]{3,2,1,0:T(8,128)(2,1)S(1)} %copy-done.2, pred[1,8,10]{2,0,1:T(4,128)(4,1)S(1)} %get-tuple-element.17, pred[1,8,10]{2,0,1:T(4,128)(4,1)S(1)} %get-tuple-element.18, pred[1,8,10]{2,0,1:T(4,128)(4,1)S(1)} %iota_compare_fusion.2), kind=kOutput, calls=%fused_computation.1 | convolution fusion | flops 287200 | bytes 85232 | tf_op jit(solution)/shard_map/dja,bdoi->bjoai/dot_general | solution.py:203
  8.6 0.1 pad_maximum_fusion.2.wst_ref
  8.7 0.1 reshape.259
  8.8 0.1 reshape.260
  8.9 0.0 collective-permute-done
  8.9 0.0 copy-done
  8.9 0.1 maximum_select_fusion
  9.0 4.0 %collective-permute-start.1 = (bf16[20,32,3]{2,1,0:T(8,128)(2,1)S(1)}, bf16[20,32,3]{2,1,0:T(8,128)(2,1)S(1)}, u32[]{:S(2)}, u32[]{:S(2)}) collective-permute-start(bf16[20,32,3]{2,1,0:T(8,128)(2,1)S(1)} %get-tuple-element.5), channel_id=1, source_target_pairs={{0,1},{1,2},{2,3},{4,5},{5,6},{6,7},{8,9},{9,10},{10,11},{12,13},{... | collective-permute-start | bytes 11528 | tf_op jit(solution)/shard_map/ppermute | solution.py:18
  13.0 1.9 %collective-permute-start.2 = (bf16[20,32,3]{2,1,0:T(8,128)(2,1)S(1)}, bf16[20,32,3]{2,1,0:T(8,128)(2,1)S(1)}, u32[]{:S(2)}, u32[]{:S(2)}) collective-permute-start(bf16[20,32,3]{2,1,0:T(8,128)(2,1)S(1)} %get-tuple-element.6), channel_id=1, source_target_pairs={{1,0},{2,1},{3,2},{5,4},{6,5},{7,6},{9,8},{10,9},{11,10},{13,12},{... | collective-permute-start | bytes 11528 | tf_op jit(solution)/shard_map/ppermute | solution.py:18
  15.0 1.0 %copy.21 = bf16[2,8,16,10,16]{2,1,4,3,0:T(8,128)(2,1)S(1)} copy(bf16[2,8,16,10,16]{4,3,2,0,1:T(8,128)(2,1)S(1)} %fusion) | data formatting | bytes 163840 | tf_op jit(solution)/shard_map/convert_element_type | solution.py:204
  16.0 0.0 copy-start.3
  16.0 0.0 copy-start.4
  16.0 0.4 %convert_element_type.88 = bf16[2,128,160]{1,2,0:T(8,128)(2,1)S(1)} reshape(bf16[2,8,16,10,16]{2,1,4,3,0:T(8,128)(2,1)S(1)} %copy.21) | data formatting | bytes 163840 | tf_op jit(solution)/shard_map/convert_element_type | solution.py:204
  16.4 0.1 copy.24.tw_ref
  16.6 0.2 convert_element_type.85.wsp_ref
  16.8 0.0 copy-done.3
  16.8 0.1 copy.25.tb_ref
  16.9 0.0 copy-done.4
  16.9 0.1 copy.23.bst_ref
  17.6 0.0 collective-permute-done.1
  17.7 2.0 %collective-permute-done.2 = bf16[20,32,3]{2,1,0:T(8,128)(2,1)S(1)} collective-permute-done((bf16[20,32,3]{2,1,0:T(8,128)(2,1)S(1)}, bf16[20,32,3]{2,1,0:T(8,128)(2,1)S(1)}, u32[]{:S(2)}, u32[]{:S(2)}) %collective-permute-start.2) | collective-permute-done | bytes 3872 | tf_op jit(solution)/shard_map/ppermute | solution.py:18
  19.7 0.4 %pad_maximum_fusion = bf16[20,38,134]{2,1,0:T(8,128)(2,1)S(1)} fusion(bf16[20,3,134]{2,1,0:T(4,128)(2,1)S(1)} %broadcast.311, bf16[20,32,3]{2,1,0:T(8,128)(2,1)S(1)} %collective-permute-done.2, bf16[16,32,128]{2,1,0:T(8,128)(2,1)S(1)} %bitcast.51, bf16[4,32,128]{2,1,0:T(8,128)(2,1)S(1)} %collective-permute-done, bf16[20,32,3]{2,1,0:T(8,128)(2,1)S(1)} %collective-permute-done.1), kind=kLoop, calls=%fused_computation.3 | loop fusion | flops 1222080 | bytes 391280 | tf_op jit(solution)/shard_map/concatenate | solution.py:39
  20.1 0.4 %convert_element_type.80 = bf16[20,5092]{1,0:T(8,128)(2,1)S(1)} reshape(bf16[20,38,134]{2,1,0:T(8,128)(2,1)S(1)} %pad_maximum_fusion) | data formatting | bytes 407360 | tf_op jit(solution)/shard_map/convert_element_type | solution.py:184
  20.6 16.3 %shard_map.82 = f32[16,5120]{1,0:T(8,128)S(1)} custom-call(s32[1]{0:T(128)} %bitcast.first_ref, f32[24,5632]{1,0:T(8,128)S(1)} %pad_convert_fusion.vp_ref, f32[2,1,5120]{2,1,0:T(1,128)S(1)} %reshape.263.mask_ref, bf16[128,160]{1,0:T(8,128)(2,1)S(1)} %pad_maximum_fusion.2.wst_ref, f32[16,1]{1,0:T(8,128)S(1)} %copy.23.bst_ref, ...), custom_call_target="tpu_custom_call" | custom-call | tf_op jit(solution)/shard_map/pallas_call | solution.py:218
  36.9 0.4 %reshape.262 = f32[16,38,134]{2,1,0:T(8,128)S(1)} reshape(f32[16,5092]{1,0:T(8,128)S(1)} %bitcast.47) | data formatting | bytes 651776 | tf_op jit(solution)/shard_map/reshape | solution.py:230
  37.3 0.8 %slice_bitcast_fusion = f32[16,1,32,128]{3,2,1,0:T(8,128)} fusion(f32[16,38,134]{2,1,0:T(8,128)S(1)} %reshape.262), kind=kLoop, calls=%fused_computation.8 | loop fusion | bytes 524288 | tf_op jit(solution)/shard_map/broadcast_in_dim | solution.py:232
  (12 shorter events, 0.2 us)
Async XLA Ops:
  0.0 7.1 %copy-start.1 = (bf16[2,9,16,16]{3,2,1,0:T(8,128)(2,1)S(1)}, bf16[2,9,16,16]{3,2,1,0:T(8,128)(2,1)}, u32[]{:S(2)}) copy-start(bf16[2,9,16,16]{3,2,1,0:T(8,128)(2,1)} %param.11) | copy-start | bytes 27652
  0.8 8.1 %collective-permute-start = (bf16[4,32,128]{2,1,0:T(8,128)(2,1)S(1)}, bf16[4,32,128]{2,1,0:T(8,128)(2,1)S(1)}, u32[]{:S(2)}, u32[]{:S(2)}) collective-permute-start(bf16[4,32,128]{2,1,0:T(8,128)(2,1)S(1)} %slice_bitcast_fusion.1), channel_id=1, source_target_pairs={{0,4},{4,8},{8,12},{12,16},{16,20},{20,24},{24,28},{1,5},{5,9},{9,... | collective-permute-start | bytes 98312 | tf_op jit(solution)/shard_map/ppermute | solution.py:18
  4.7 3.3 %copy-start.2 = (bf16[2,3,16,16]{3,2,1,0:T(8,128)(2,1)S(1)}, bf16[2,3,16,16]{3,2,1,0:T(8,128)(2,1)}, u32[]{:S(2)}) copy-start(bf16[2,3,16,16]{3,2,1,0:T(8,128)(2,1)} %param.12) | copy-start | bytes 9220
  7.2 1.7 %copy-start = (bf16[16,1,32,128]{3,2,1,0:T(8,128)(2,1)S(1)}, bf16[16,1,32,128]{3,2,1,0:T(8,128)(2,1)}, u32[]{:S(2)}) copy-start(bf16[16,1,32,128]{3,2,1,0:T(8,128)(2,1)} %param.8) | copy-start | bytes 393220
  9.0 8.6 %collective-permute-start.1 = (bf16[20,32,3]{2,1,0:T(8,128)(2,1)S(1)}, bf16[20,32,3]{2,1,0:T(8,128)(2,1)S(1)}, u32[]{:S(2)}, u32[]{:S(2)}) collective-permute-start(bf16[20,32,3]{2,1,0:T(8,128)(2,1)S(1)} %get-tuple-element.5), channel_id=1, source_target_pairs={{0,1},{1,2},{2,3},{4,5},{5,6},{6,7},{8,9},{9,10},{10,11},{12,13},{... | collective-permute-start | bytes 11528 | tf_op jit(solution)/shard_map/ppermute | solution.py:18
  13.0 6.6 %collective-permute-start.2 = (bf16[20,32,3]{2,1,0:T(8,128)(2,1)S(1)}, bf16[20,32,3]{2,1,0:T(8,128)(2,1)S(1)}, u32[]{:S(2)}, u32[]{:S(2)}) collective-permute-start(bf16[20,32,3]{2,1,0:T(8,128)(2,1)S(1)} %get-tuple-element.6), channel_id=1, source_target_pairs={{1,0},{2,1},{3,2},{5,4},{6,5},{7,6},{9,8},{10,9},{11,10},{13,12},{... | collective-permute-start | bytes 11528 | tf_op jit(solution)/shard_map/ppermute | solution.py:18
  16.0 0.8 %copy-start.3 = (f32[2,16]{1,0:T(2,128)S(1)}, f32[2,16]{1,0:T(2,128)}, u32[]{:S(2)}) copy-start(f32[2,16]{1,0:T(2,128)} %param.13) | copy-start | bytes 388
  16.0 0.9 %copy-start.4 = (f32[16]{0:T(128)S(1)}, f32[16]{0:T(128)}, u32[]{:S(2)}) copy-start(f32[16]{0:T(128)} %param.10) | copy-start | bytes 196

commit v8 on v7

--- a/solution.py
+++ b/solution.py
@@ -185,7 +185,7 @@
     vp = flat
 
     channels = stem_weight.shape[1]
-    w_hi = stem_weight.astype(jnp.bfloat16).astype(jnp.float32)
+    w_hi = lax.reduce_precision(stem_weight, exponent_bits=8, mantissa_bits=7)
     w_lo = stem_weight - w_hi
     eye = jnp.eye(8, dtype=jnp.float32)
 
@@ -203,7 +203,7 @@
     tw = jnp.einsum("dja,bdoi->bjoai", band, temporal_weight.astype(jnp.float32))
     tw = tw.reshape(2, 8 * channels, 10 * channels).astype(jnp.bfloat16)
     tb = temporal_bias.astype(jnp.float32)[:, :, None]
-    hw_hi = head_weight.astype(jnp.bfloat16).astype(jnp.float32)
+    hw_hi = lax.reduce_precision(head_weight.astype(jnp.float32), exponent_bits=8, mantissa_bits=7)
     hw_lo = head_weight - hw_hi
     frame_eye = jnp.eye(8, dtype=jnp.float32)
     hw = jnp.concatenate([jnp.einsum("jk,c->jkc", frame_eye, w).reshape(8, 8 * channels) for w in (hw_hi, hw_lo)], axis=1)

time: 38.4 us -> 38.3 us (level)
    reduce_precision x0 -> x2, other arithmetic: none -> 1.37 us  [the longest x1 0.7 us: shards(): w_hi = lax.reduce_precision(stem_weight, exponent_bits=8, mantissa_bits=7)]
    convert_element_type x1 -> x0, other arithmetic: 0.78 us -> none  [shards(): w_hi = stem_weight.astype(jnp.bfloat16).astype(jnp.float32)]
    another operation x4 -> x3, other arithmetic: 0.83 us -> 0.09 us
  transfers between devices with their start and end apart: 3 -> 3, of which waited for: 1 -> 1; matrix products, arithmetic and copies ran while one was open for 16% -> 15% of each run, Pallas kernels for 0% -> 0%
where the time goes in v8:
time: 38.3 us; the launch traced here: 38 us
  Pallas kernels  16.3 us (43%)
  starting transfers between devices  9.84 us (26%)
  local copies, waits for them, and re-layouts  5.35 us (14%)
  other arithmetic  2.91 us (8%)
  waiting for transfers between devices  2.03 us (5%)
  between operations  0.99 us (3%)
  matrix products  0.53 us (1%)
    pallas_call x1, Pallas kernels, shards(): pl.pallas_call(make_kernel(n_in, count, pitch, length, base, total, heigh...  16.3 us
    ppermute x3, starting transfers between devices, shifted(): lax.ppermute(value, axis, [(source, source + steps) for source in range(l...  9.84 us
    ppermute x3, waiting for transfers between devices, shifted(): lax.ppermute(value, axis, [(source, source + steps) for source in range(l...  2.03 us
    convert_element_type x3, local copies, waits for them, and re-layouts, shards(): tw = tw.reshape(2, 8 * channels, 10 * channels).astype(jnp.bfloat16)  1.49 us
    broadcast_in_dim x1, local copies, waits for them, and re-layouts, shards(): return result[:, None]  0.84 us
    slice x1, local copies, waits for them, and re-layouts, shards(): lead = shifted(clip[-LEAD:], 'tm', 1)  0.79 us
  transfers between devices with their start and end apart: 3, of which 1 were waited for; matrix products, arithmetic and copies ran while one was open for 15% of the time, Pallas kernels for 0%

profile of v8, /device:TPU:1, one launch (start us, length us, event | category | flops | bytes accessed | tf_op | source)
XLA Modules:
  0.0 38.0 jit_solution(15999419735121684910)
XLA Ops:
  0.0 0.0 copy-start.1
  0.0 0.8 %slice_bitcast_fusion.1 = bf16[4,32,128]{2,1,0:T(8,128)(2,1)S(1)} fusion(bf16[16,1,32,128]{3,2,0,1:T(8,128)(2,1)} %bitcast.49), kind=kLoop, calls=%fused_computation.25 | loop fusion | bytes 65536 | tf_op jit(solution)/shard_map/slice | solution.py:174
  0.8 3.9 %collective-permute-start = (bf16[4,32,128]{2,1,0:T(8,128)(2,1)S(1)}, bf16[4,32,128]{2,1,0:T(8,128)(2,1)S(1)}, u32[]{:S(2)}, u32[]{:S(2)}) collective-permute-start(bf16[4,32,128]{2,1,0:T(8,128)(2,1)S(1)} %slice_bitcast_fusion.1), channel_id=1, source_target_pairs={{0,4},{4,8},{8,12},{12,16},{16,20},{20,24},{24,28},{1,5},{5,9},{9,... | collective-permute-start | bytes 98312 | tf_op jit(solution)/shard_map/ppermute | solution.py:18
  4.7 0.0 copy-start.2
  4.8 0.7 %fusion.16 = (f32[9,16]{1,0:T(8,128)S(1)}, f32[9,16]{1,0:T(8,128)S(1)}) fusion(f32[9,16]{1,0:T(8,128)} %param.9), kind=kLoop, calls=%fused_computation.50 | loop fusion | flops 288 | bytes 1728 | tf_op jit(solution)/shard_map/reduce_precision | solution.py:188
  5.6 0.1 copy.22
  5.6 0.1 fusion.2
  5.8 0.1 reshape.255
  5.9 0.1 copy.17
  6.0 0.2 reshape.256
  6.2 0.1 copy.18
  6.3 0.7 %fusion.17 = (f32[16]{0:T(128)S(1)}, f32[16]{0:T(128)S(1)}) fusion(f32[16]{0:T(128)} %param.14), kind=kLoop, calls=%fused_computation.51 | loop fusion | flops 32 | bytes 192 | tf_op jit(solution)/shard_map/reduce_precision | solution.py:206
  7.0 0.0 copy-done.1
  7.0 0.0 copy-start
  7.0 0.1 reshape.264
  7.2 0.3 compare_and_fusion
  7.5 0.1 add_convert_fusion
  7.6 0.1 iota_compare_fusion
  7.6 0.2 fusion.1
  7.8 0.1 multiply_convert_fusion.4
  7.9 0.0 copy-done.2
  7.9 0.5 %fusion = bf16[2,8,16,10,16]{4,3,2,0,1:T(8,128)(2,1)S(1)} fusion(bf16[2,3,16,16]{3,2,1,0:T(8,128)(2,1)S(1)} %copy-done.2, pred[1,8,10]{2,0,1:T(4,128)(4,1)S(1)} %get-tuple-element.17, pred[1,8,10]{2,0,1:T(4,128)(4,1)S(1)} %get-tuple-element.18, pred[1,8,10]{2,0,1:T(4,128)(4,1)S(1)} %iota_compare_fusion.2), kind=kOutput, calls=%fused_computation.1 | convolution fusion | flops 287200 | bytes 85232 | tf_op jit(solution)/shard_map/dja,bdoi->bjoai/dot_general | solution.py:203
  8.5 0.1 pad_maximum_fusion.2.wst_ref
  8.6 0.1 reshape.259
  8.7 0.1 reshape.260
  8.8 0.0 collective-permute-done
  8.8 0.0 copy-done
  8.8 0.1 maximum_select_fusion
  8.9 4.0 %collective-permute-start.1 = (bf16[20,32,3]{2,1,0:T(8,128)(2,1)S(1)}, bf16[20,32,3]{2,1,0:T(8,128)(2,1)S(1)}, u32[]{:S(2)}, u32[]{:S(2)}) collective-permute-start(bf16[20,32,3]{2,1,0:T(8,128)(2,1)S(1)} %get-tuple-element.5), channel_id=1, source_target_pairs={{0,1},{1,2},{2,3},{4,5},{5,6},{6,7},{8,9},{9,10},{10,11},{12,13},{... | collective-permute-start | bytes 11528 | tf_op jit(solution)/shard_map/ppermute | solution.py:18
  12.9 1.9 %collective-permute-start.2 = (bf16[20,32,3]{2,1,0:T(8,128)(2,1)S(1)}, bf16[20,32,3]{2,1,0:T(8,128)(2,1)S(1)}, u32[]{:S(2)}, u32[]{:S(2)}) collective-permute-start(bf16[20,32,3]{2,1,0:T(8,128)(2,1)S(1)} %get-tuple-element.6), channel_id=1, source_target_pairs={{1,0},{2,1},{3,2},{5,4},{6,5},{7,6},{9,8},{10,9},{11,10},{13,12},{... | collective-permute-start | bytes 11528 | tf_op jit(solution)/shard_map/ppermute | solution.py:18
  14.9 1.0 %copy.21 = bf16[2,8,16,10,16]{2,1,4,3,0:T(8,128)(2,1)S(1)} copy(bf16[2,8,16,10,16]{4,3,2,0,1:T(8,128)(2,1)S(1)} %fusion) | data formatting | bytes 163840 | tf_op jit(solution)/shard_map/convert_element_type | solution.py:204
  15.8 0.0 copy-start.3
  15.8 0.0 copy-start.4
  15.9 0.4 %convert_element_type.76 = bf16[2,128,160]{1,2,0:T(8,128)(2,1)S(1)} reshape(bf16[2,8,16,10,16]{2,1,4,3,0:T(8,128)(2,1)S(1)} %copy.21) | data formatting | bytes 163840 | tf_op jit(solution)/shard_map/convert_element_type | solution.py:204
  16.3 0.1 copy.24.tw_ref
  16.4 0.2 convert_element_type.73.wsp_ref
  16.6 0.0 copy-done.3
  16.7 0.1 copy.25.tb_ref
  16.7 0.0 copy-done.4
  16.7 0.1 copy.23.bst_ref
  17.5 0.0 collective-permute-done.1
  17.5 2.0 %collective-permute-done.2 = bf16[20,32,3]{2,1,0:T(8,128)(2,1)S(1)} collective-permute-done((bf16[20,32,3]{2,1,0:T(8,128)(2,1)S(1)}, bf16[20,32,3]{2,1,0:T(8,128)(2,1)S(1)}, u32[]{:S(2)}, u32[]{:S(2)}) %collective-permute-start.2) | collective-permute-done | bytes 3872 | tf_op jit(solution)/shard_map/ppermute | solution.py:18
  19.5 0.4 %pad_maximum_fusion = bf16[20,38,134]{2,1,0:T(8,128)(2,1)S(1)} fusion(bf16[20,3,134]{2,1,0:T(4,128)(2,1)S(1)} %broadcast.311, bf16[20,32,3]{2,1,0:T(8,128)(2,1)S(1)} %collective-permute-done.2, bf16[16,32,128]{2,1,0:T(8,128)(2,1)S(1)} %bitcast.51, bf16[4,32,128]{2,1,0:T(8,128)(2,1)S(1)} %collective-permute-done, bf16[20,32,3]{2,1,0:T(8,128)(2,1)S(1)} %collective-permute-done.1), kind=kLoop, calls=%fused_computation.3 | loop fusion | flops 1222080 | bytes 391280 | tf_op jit(solution)/shard_map/concatenate | solution.py:39
  20.0 0.4 %convert_element_type.70 = bf16[20,5092]{1,0:T(8,128)(2,1)S(1)} reshape(bf16[20,38,134]{2,1,0:T(8,128)(2,1)S(1)} %pad_maximum_fusion) | data formatting | bytes 407360 | tf_op jit(solution)/shard_map/convert_element_type | solution.py:184
  20.4 16.3 %shard_map.82 = f32[16,5120]{1,0:T(8,128)S(1)} custom-call(s32[1]{0:T(128)} %bitcast.first_ref, f32[24,5632]{1,0:T(8,128)S(1)} %pad_convert_fusion.vp_ref, f32[2,1,5120]{2,1,0:T(1,128)S(1)} %reshape.263.mask_ref, bf16[128,160]{1,0:T(8,128)(2,1)S(1)} %pad_maximum_fusion.2.wst_ref, f32[16,1]{1,0:T(8,128)S(1)} %copy.23.bst_ref, ...), custom_call_target="tpu_custom_call" | custom-call | tf_op jit(solution)/shard_map/pallas_call | solution.py:218
  36.7 0.4 %reshape.262 = f32[16,38,134]{2,1,0:T(8,128)S(1)} reshape(f32[16,5092]{1,0:T(8,128)S(1)} %bitcast.47) | data formatting | bytes 651776 | tf_op jit(solution)/shard_map/reshape | solution.py:230
  37.1 0.8 %slice_bitcast_fusion = f32[16,1,32,128]{3,2,1,0:T(8,128)} fusion(f32[16,38,134]{2,1,0:T(8,128)S(1)} %reshape.262), kind=kLoop, calls=%fused_computation.8 | loop fusion | bytes 524288 | tf_op jit(solution)/shard_map/broadcast_in_dim | solution.py:232
  (12 shorter events, 0.2 us)
Async XLA Ops:
  0.0 7.0 %copy-start.1 = (bf16[2,9,16,16]{3,2,1,0:T(8,128)(2,1)S(1)}, bf16[2,9,16,16]{3,2,1,0:T(8,128)(2,1)}, u32[]{:S(2)}) copy-start(bf16[2,9,16,16]{3,2,1,0:T(8,128)(2,1)} %param.11) | copy-start | bytes 27652
  0.8 8.0 %collective-permute-start = (bf16[4,32,128]{2,1,0:T(8,128)(2,1)S(1)}, bf16[4,32,128]{2,1,0:T(8,128)(2,1)S(1)}, u32[]{:S(2)}, u32[]{:S(2)}) collective-permute-start(bf16[4,32,128]{2,1,0:T(8,128)(2,1)S(1)} %slice_bitcast_fusion.1), channel_id=1, source_target_pairs={{0,4},{4,8},{8,12},{12,16},{16,20},{20,24},{24,28},{1,5},{5,9},{9,... | collective-permute-start | bytes 98312 | tf_op jit(solution)/shard_map/ppermute | solution.py:18
  4.7 3.2 %copy-start.2 = (bf16[2,3,16,16]{3,2,1,0:T(8,128)(2,1)S(1)}, bf16[2,3,16,16]{3,2,1,0:T(8,128)(2,1)}, u32[]{:S(2)}) copy-start(bf16[2,3,16,16]{3,2,1,0:T(8,128)(2,1)} %param.12) | copy-start | bytes 9220
  7.0 1.7 %copy-start = (bf16[16,1,32,128]{3,2,1,0:T(8,128)(2,1)S(1)}, bf16[16,1,32,128]{3,2,1,0:T(8,128)(2,1)}, u32[]{:S(2)}) copy-start(bf16[16,1,32,128]{3,2,1,0:T(8,128)(2,1)} %param.8) | copy-start | bytes 393220
  8.9 8.6 %collective-permute-start.1 = (bf16[20,32,3]{2,1,0:T(8,128)(2,1)S(1)}, bf16[20,32,3]{2,1,0:T(8,128)(2,1)S(1)}, u32[]{:S(2)}, u32[]{:S(2)}) collective-permute-start(bf16[20,32,3]{2,1,0:T(8,128)(2,1)S(1)} %get-tuple-element.5), channel_id=1, source_target_pairs={{0,1},{1,2},{2,3},{4,5},{5,6},{6,7},{8,9},{9,10},{10,11},{12,13},{... | collective-permute-start | bytes 11528 | tf_op jit(solution)/shard_map/ppermute | solution.py:18
  12.9 6.6 %collective-permute-start.2 = (bf16[20,32,3]{2,1,0:T(8,128)(2,1)S(1)}, bf16[20,32,3]{2,1,0:T(8,128)(2,1)S(1)}, u32[]{:S(2)}, u32[]{:S(2)}) collective-permute-start(bf16[20,32,3]{2,1,0:T(8,128)(2,1)S(1)} %get-tuple-element.6), channel_id=1, source_target_pairs={{1,0},{2,1},{3,2},{5,4},{6,5},{7,6},{9,8},{10,9},{11,10},{13,12},{... | collective-permute-start | bytes 11528 | tf_op jit(solution)/shard_map/ppermute | solution.py:18
  15.8 0.8 %copy-start.3 = (f32[2,16]{1,0:T(2,128)S(1)}, f32[2,16]{1,0:T(2,128)}, u32[]{:S(2)}) copy-start(f32[2,16]{1,0:T(2,128)} %param.13) | copy-start | bytes 388
  15.8 0.9 %copy-start.4 = (f32[16]{0:T(128)S(1)}, f32[16]{0:T(128)}, u32[]{:S(2)}) copy-start(f32[16]{0:T(128)} %param.10) | copy-start | bytes 196
